TPU v7x, 1024 devices: a whole 4x8x16 slice. The times are simulated.
1024 devices in a mesh: ctx: 128 (over x, z, y_lo), dp: 8 (over y_hi, core).
Axes of the slice: x: 4, y: 8 (y_hi: 4, y_lo: 2; y = y_hi * 2 + y_lo), z: 16, core: 2. Of those that a mesh axis runs over, the one named last changes fastest.
Arguments:
- queries: bfloat16 [8, 16384, 2048], P('dp', 'ctx'), may hold values from -400 to 400
- keys: bfloat16 [8, 16384, 1024], P('dp', 'ctx'), may hold values from -400 to 400
- values: bfloat16 [8, 16384, 1024], P('dp', 'ctx'), may hold values from -6 to 6
- q_gain: float32 [256], replicated, may hold values from 0.25 to 1.75
- key_norm_gain: float32 [256], replicated, may hold values from 0.25 to 1.75
- segment_ids: int32 [8, 16384], P('dp', 'ctx'), may hold values from 0 to 63, never falling along the last dimension, each value on 1 to 1024 neighbouring positions
- output_gradient: bfloat16 [8, 16384, 2048], P('dp', 'ctx'), may hold values from -14 to 14
Outputs:
- attn_out: bfloat16 [8, 16384, 2048], P('dp', 'ctx')
- grad_queries: bfloat16 [8, 16384, 2048], P('dp', 'ctx')
- key_gradient: bfloat16 [8, 16384, 1024], P('dp', 'ctx')
- value_gradient: bfloat16 [8, 16384, 1024], P('dp', 'ctx')
- grad_q_gain: float32 [256], replicated
- grad_k_gain: float32 [256], replicated
Inputs may be any that keep to these rules, and one draw needn't show every extreme that they name: `segment_ids`: document ids never fall along a sequence; every id from 0 to 63 is used, each document holds 1 to 1024 tokens and at least one holds exactly 1024.
All inputs are finite; a program needn't handle non-finite values.
Results may differ from a plain program's by a relative error of at most 0.013.
Values may be sent and summed in bfloat16 or wider, within the bound.
No kernel may reach another device: no remote copies, remote signals or barrier semaphores. Data moves between devices by JAX's collectives and lax.ppermute only.
A program may use at most 32 MiB of HBM per device.

v0:
```python
import jax
import jax.numpy as jnp
from jax import lax
from jax.sharding import PartitionSpec as P

QUERY_HEADS = 8
KEY_VALUE_HEADS = 4
HEAD_SIZE = 256
WINDOW = 256
HALO = 2


EPS = 1e-06


def shifted(value, axis, by):
    count = lax.axis_size(axis)
    pairs = [(i, i + by) for i in range(count) if 0 <= i + by < count]
    return lax.ppermute(value, axis, pairs)


def rms_normalize(inputs, heads, gain_vec):
    as_float = inputs.astype(jnp.float32).reshape(inputs.shape[0], heads, HEAD_SIZE)
    inv_rms = lax.rsqrt(jnp.mean(as_float * as_float, -1, keepdims=True) + EPS)
    normed = as_float * inv_rms
    return (normed, inv_rms, (normed * gain_vec).astype(jnp.bfloat16))


def rms_norm_backward(upstream, normed, inv_rms, gain_vec):
    scaled = upstream * gain_vec
    return inv_rms * (scaled - normed * jnp.mean(scaled * normed, -1, keepdims=True))


def body(queries, keys, values, q_gain, key_norm_gain, segment_ids, output_gradient):
    token_rows = queries.shape[1]
    query_group_width = QUERY_HEADS // KEY_VALUE_HEADS
    score_scale = HEAD_SIZE ** (-0.5)
    ctx_index = lax.axis_index("ctx")
    q_normed, q_inv, query_norm_result = rms_normalize(queries[0], QUERY_HEADS, q_gain)
    normalized_keys, key_inverse_rms, key_norm_result = rms_normalize(
        keys[0], KEY_VALUE_HEADS, key_norm_gain
    )
    own_seg = segment_ids[0]
    local_key_value = jnp.stack(
        [key_norm_result.reshape(token_rows, KEY_VALUE_HEADS * HEAD_SIZE), values[0]]
    )
    received = []
    for offset in range(1, HALO + 1):
        received.append(shifted((local_key_value, own_seg), "ctx", offset))
    blocks = [received[HALO - 1 - block] for block in range(HALO)] + [(local_key_value, own_seg)]
    positions = jnp.arange(token_rows, dtype=jnp.int32)
    q_pos = ctx_index * token_rows + positions
    grouped_queries = query_norm_result.reshape(
        token_rows, KEY_VALUE_HEADS, query_group_width, HEAD_SIZE
    )
    key_block_list, value_block_list, key_masks, live_flags = ([], [], [], [])
    for block in range(HALO + 1):
        key_value_pair, seg_block = blocks[block]
        k_pos = (ctx_index - HALO + block) * token_rows + positions
        distance = q_pos[:, None] - k_pos[None, :]
        key_mask = (
            (distance >= 0)
            & (distance < WINDOW)
            & (k_pos[None, :] >= 0)
            & (own_seg[:, None] == seg_block[None, :])
        )
        key_block_list.append(key_value_pair[0].reshape(token_rows, KEY_VALUE_HEADS, HEAD_SIZE))
        value_block_list.append(key_value_pair[1].reshape(token_rows, KEY_VALUE_HEADS, HEAD_SIZE))
        key_masks.append(key_mask)
        live_flags.append(jnp.any(key_mask))
    output_shape = (token_rows, KEY_VALUE_HEADS, query_group_width, HEAD_SIZE)

    def exp_block(block):
        scores = (
            jnp.einsum(
                "qhgd,khd->hgqk",
                grouped_queries,
                key_block_list[block],
                preferred_element_type=jnp.float32,
            )
            * score_scale
        )
        return jnp.where(key_masks[block], jnp.exp(scores), 0.0)

    exp_blocks = [exp_block(block) for block in range(HALO + 1)]
    row_totals = sum((jnp.sum(exp_value, -1) for exp_value in exp_blocks))[..., None]
    prob_b_blocks = [(exp_value / row_totals).astype(jnp.bfloat16) for exp_value in exp_blocks]

    def attend_block(block):
        return jnp.einsum(
            "hgqk,khd->qhgd",
            prob_b_blocks[block],
            value_block_list[block],
            preferred_element_type=jnp.float32,
        )

    attn_sum = sum((attend_block(block) for block in range(HALO + 1)))
    attn_out = attn_sum.astype(jnp.bfloat16)
    grad_out = output_gradient[0].reshape(output_shape)
    row_delta = jnp.sum(grad_out.astype(jnp.float32) * attn_out.astype(jnp.float32), -1).transpose(
        1, 2, 0
    )

    def backward_block(block):
        prob_grad = jnp.einsum(
            "qhgd,khd->hgqk", grad_out, value_block_list[block], preferred_element_type=jnp.float32
        )
        score_grad = (exp_blocks[block] / row_totals * (prob_grad - row_delta[..., None])).astype(
            jnp.bfloat16
        )
        q_part = jnp.einsum(
            "hgqk,khd->qhgd", score_grad, key_block_list[block], preferred_element_type=jnp.float32
        )
        key_term = (
            jnp.einsum(
                "hgqk,qhgd->khd", score_grad, grouped_queries, preferred_element_type=jnp.float32
            )
            * score_scale
        ).astype(jnp.bfloat16)
        value_term = jnp.einsum(
            "hgqk,qhgd->khd", prob_b_blocks[block], grad_out, preferred_element_type=jnp.float32
        ).astype(jnp.bfloat16)
        return (q_part, key_term, value_term)

    back_blocks = [backward_block(block) for block in range(HALO + 1)]
    q_grad_norm = (sum((item[0] for item in back_blocks)) * score_scale).reshape(
        token_rows, QUERY_HEADS, HEAD_SIZE
    )
    key_acc = back_blocks[HALO][1].astype(jnp.float32)
    value_accumulator = back_blocks[HALO][2].astype(jnp.float32)
    for offset in range(1, HALO + 1):
        block = HALO - offset
        returned = shifted(
            jnp.stack([back_blocks[block][1], back_blocks[block][2]]), "ctx", -offset
        )
        key_acc = key_acc + returned[0].astype(jnp.float32)
        value_accumulator = value_accumulator + returned[1].astype(jnp.float32)
    grad_queries = (
        rms_norm_backward(q_grad_norm, q_normed, q_inv, q_gain)
        .astype(jnp.bfloat16)
        .reshape(1, token_rows, QUERY_HEADS * HEAD_SIZE)
    )
    key_gradient = (
        rms_norm_backward(key_acc, normalized_keys, key_inverse_rms, key_norm_gain)
        .astype(jnp.bfloat16)
        .reshape(1, token_rows, KEY_VALUE_HEADS * HEAD_SIZE)
    )
    value_gradient = value_accumulator.astype(jnp.bfloat16).reshape(
        1, token_rows, KEY_VALUE_HEADS * HEAD_SIZE
    )
    q_sum_part = jnp.sum(q_grad_norm * q_normed, (0, 1))
    k_sum_part = jnp.sum(key_acc * normalized_keys, (0, 1))
    q_total, k_total = lax.psum((q_sum_part, k_sum_part), ("ctx", "dp"))
    factor = (lax.axis_size("ctx") * lax.axis_size("dp") * token_rows) ** (-0.5)
    return (
        attn_out.reshape(1, token_rows, QUERY_HEADS * HEAD_SIZE),
        grad_queries,
        key_gradient,
        value_gradient,
        q_total * factor,
        k_total * factor,
    )


def solution(mesh):
    placed = (
        P("dp", "ctx", None),
        P("dp", "ctx", None),
        P("dp", "ctx", None),
        P(),
        P(),
        P("dp", "ctx"),
        P("dp", "ctx", None),
    )
    return jax.shard_map(
        body,
        mesh=mesh,
        in_specs=placed,
        out_specs=(
            P("dp", "ctx", None),
            P("dp", "ctx", None),
            P("dp", "ctx", None),
            P("dp", "ctx", None),
            P(),
            P(),
        ),
        check_vma=False,
    )
```

profile of v0, /device:TPU:1, one launch (start us, length us, event | category | flops | bytes accessed | tf_op | source)
XLA Modules:
  0.0 211.1 jit_solution(10943828354925070417)
XLA Ops:
  1.3 4.8 %collective-permute-start.1 = (s32[128]{0:T(128)S(1)}, s32[128]{0:T(128)S(1)}, u32[]{:S(2)}, u32[]{:S(2)}) collective-permute-start(s32[128]{0:T(128)S(1)} %bitcast.294), channel_id=1, source_target_pairs={{0,16},{8,24},{16,32},{24,40},{32,48},{40,56},{48,64},{56,72},{64,... | collective-permute-start | bytes 1544 | tf_op jit(solution)/shard_map/ppermute | solution.py:19
  6.1 3.2 %collective-permute-start.2 = (s32[128]{0:T(128)S(1)}, s32[128]{0:T(128)S(1)}, u32[]{:S(2)}, u32[]{:S(2)}) collective-permute-start(s32[128]{0:T(128)S(1)} %bitcast.295), channel_id=1, source_target_pairs={{0,8},{8,16},{16,24},{24,32},{32,40},{40,48},{48,56},{56,64},{64,7... | collective-permute-start | bytes 1544 | tf_op jit(solution)/shard_map/ppermute | solution.py:19
  12.6 4.8 %collective-permute-start = (bf16[2,128,1024]{1,2,0:T(8,128)(2,1)}, bf16[2,128,1024]{1,2,0:T(8,128)(2,1)}, u32[]{:S(2)}, u32[]{:S(2)}) collective-permute-start(bf16[2,128,1024]{1,2,0:T(8,128)(2,1)} %pad_maximum_fusion), channel_id=1, source_target_pairs={{0,16},{8,24},{16,32},{24,40},{32,48},{40,56},{48,64},{56,72},{64,... | collective-permute-start | bytes 1572872 | tf_op jit(solution)/shard_map/ppermute | solution.py:19
  17.4 4.7 %collective-permute-start.3 = (bf16[2,128,1024]{1,2,0:T(8,128)(2,1)}, bf16[2,128,1024]{1,2,0:T(8,128)(2,1)}, u32[]{:S(2)}, u32[]{:S(2)}) collective-permute-start(bf16[2,128,1024]{1,2,0:T(8,128)(2,1)} %pad_maximum_fusion), channel_id=1, source_target_pairs={{0,8},{8,16},{16,24},{24,32},{32,40},{40,48},{48,56},{56,64},{64,7... | collective-permute-start | bytes 1572872 | tf_op jit(solution)/shard_map/ppermute | solution.py:19
  23.9 2.6 %copy.265 = f32[16,8,8,256]{3,2,1,0:T(8,128)} copy(f32[16,8,8,256]{3,1,2,0:T(8,128)} %bitcast.250) | data formatting | bytes 2097152
  26.5 1.4 reduce_sum.91
  28.5 1.3 copy.186
  29.8 1.2 mul.241
  31.1 2.4 %mul.242 = f32[1,128,2048]{2,1,0:T(8,128)} reshape(f32[128,8,256]{2,1,0:T(8,128)} %mul.241) | data formatting | bytes 2097152 | tf_op jit(solution)/shard_map/mul | solution.py:25
  34.1 1.3 fusion.69
  38.1 1.2 multiply_reduce_fusion
  41.9 1.3 collective-permute-start.4
  44.3 1.3 collective-permute-start.5
  46.0 1.5 fusion.38
  47.7 1.2 mul.262
  48.9 1.3 broadcast_multiply_fusion
  50.2 1.3 copy.196
  51.6 2.1 %copy.207 = bf16[1,128,2048]{2,1,0:T(8,128)(2,1)} copy(bf16[1,128,2048]{1,2,0:T(8,128)(2,1)} %bitcast.265) | data formatting | bytes 1048576
  53.7 2.7 %multiply_convert_fusion = bf16[1,128,2048]{2,1,0:T(8,128)(2,1)} fusion(f32[1,128,2048]{2,1,0:T(8,128)S(1)} %copy-done.1, f32[1,128,2048]{2,1,0:T(8,128)} %mul.262, f32[1,128,2048]{2,1,0:T(8,128)} %copy.196, bf16[1,128,2048]{2,1,0:T(8,128)(2,1)S(1)} %copy-done, f32[2048]{0:T(1024)S(1)} %bitcast.276), kind=kLoop, calls=%fused_computation.56 | loop fusion | flops 1835008 | bytes 4202496 | tf_op jit(solution)/shard_map/convert_element_type | solution.py:140
  56.4 7.2 %collective-permute-done.4 = bf16[2,128,4,256]{1,3,2,0:T(8,128)(2,1)} collective-permute-done((bf16[2,128,4,256]{1,3,2,0:T(8,128)(2,1)}, bf16[2,128,4,256]{1,3,2,0:T(8,128)(2,1)}, u32[]{:S(2)}, u32[]{:S(2)}) %collective-permute-start.4) | collective-permute-done | bytes 524320 | tf_op jit(solution)/shard_map/ppermute | solution.py:19
  63.6 8.3 %collective-permute-done.5 = bf16[2,128,4,256]{1,3,2,0:T(8,128)(2,1)} collective-permute-done((bf16[2,128,4,256]{1,3,2,0:T(8,128)(2,1)}, bf16[2,128,4,256]{1,3,2,0:T(8,128)(2,1)}, u32[]{:S(2)}, u32[]{:S(2)}) %collective-permute-start.5) | collective-permute-done | bytes 524320 | tf_op jit(solution)/shard_map/ppermute | solution.py:19
  71.9 1.5 multiply_reduce_fusion.1
  73.4 133.4 %all-reduce = (f32[256]{0:T(256)S(1)}, f32[256]{0:T(256)S(1)}) all-reduce(f32[256]{0:T(256)S(1)} %get-tuple-element.36, f32[256]{0:T(256)S(1)} %get-tuple-element.38), channel_id=1, replica_groups=mesh['ctx'=128,'dp'=8] {'ctx','dp'}, use_global_device_ids=true, to_apply=%region_9.10 | all-reduce | flops 512 | bytes 4096 | tf_op jit(solution)/shard_map/psum | solution.py:153
  207.9 1.3 fusion.39
  (74 shorter events, 16.9 us)
Async XLA Ops:
  0.6 0.7 copy-start.9
  1.3 32.2 %collective-permute-start.1 = (s32[128]{0:T(128)S(1)}, s32[128]{0:T(128)S(1)}, u32[]{:S(2)}, u32[]{:S(2)}) collective-permute-start(s32[128]{0:T(128)S(1)} %bitcast.294), channel_id=1, source_target_pairs={{0,16},{8,24},{16,32},{24,40},{32,48},{40,56},{48,64},{56,72},{64,... | collective-permute-start | bytes 1544 | tf_op jit(solution)/shard_map/ppermute | solution.py:19
  6.1 27.4 %collective-permute-start.2 = (s32[128]{0:T(128)S(1)}, s32[128]{0:T(128)S(1)}, u32[]{:S(2)}, u32[]{:S(2)}) collective-permute-start(s32[128]{0:T(128)S(1)} %bitcast.295), channel_id=1, source_target_pairs={{0,8},{8,16},{16,24},{24,32},{32,40},{40,48},{48,56},{56,64},{64,7... | collective-permute-start | bytes 1544 | tf_op jit(solution)/shard_map/ppermute | solution.py:19
  10.4 1.0 copy-start.2
  10.5 0.7 copy-start.7
  11.8 10.3 %copy-start = (bf16[1,128,2048]{2,1,0:T(8,128)(2,1)S(1)}, bf16[1,128,2048]{2,1,0:T(8,128)(2,1)}, u32[]{:S(2)}) copy-start(bf16[1,128,2048]{2,1,0:T(8,128)(2,1)} %param.7) | copy-start | bytes 1572868
  12.6 21.5 %collective-permute-start = (bf16[2,128,1024]{1,2,0:T(8,128)(2,1)}, bf16[2,128,1024]{1,2,0:T(8,128)(2,1)}, u32[]{:S(2)}, u32[]{:S(2)}) collective-permute-start(bf16[2,128,1024]{1,2,0:T(8,128)(2,1)} %pad_maximum_fusion), channel_id=1, source_target_pairs={{0,16},{8,24},{16,32},{24,40},{32,48},{40,56},{48,64},{56,72},{64,... | collective-permute-start | bytes 1572872 | tf_op jit(solution)/shard_map/ppermute | solution.py:19
  17.4 18.3 %collective-permute-start.3 = (bf16[2,128,1024]{1,2,0:T(8,128)(2,1)}, bf16[2,128,1024]{1,2,0:T(8,128)(2,1)}, u32[]{:S(2)}, u32[]{:S(2)}) collective-permute-start(bf16[2,128,1024]{1,2,0:T(8,128)(2,1)} %pad_maximum_fusion), channel_id=1, source_target_pairs={{0,8},{8,16},{16,24},{24,32},{32,40},{40,48},{48,56},{56,64},{64,7... | collective-permute-start | bytes 1572872 | tf_op jit(solution)/shard_map/ppermute | solution.py:19
  23.2 0.7 copy-start.8
  34.1 6.0 %copy-start.3 = (f32[4,2,128,128]{2,3,1,0:T(8,128)}, f32[4,2,128,128]{2,3,1,0:T(8,128)S(1)}, u32[]{:S(2)}) copy-start(f32[4,2,128,128]{2,3,1,0:T(8,128)S(1)} %get-tuple-element.52) | copy-start | bytes 1572868
  40.4 5.2 %copy-start.5 = (bf16[4,2,128,128]{2,3,1,0:T(8,128)(2,1)}, bf16[4,2,128,128]{2,3,1,0:T(8,128)(2,1)S(1)}, u32[]{:S(2)}) copy-start(bf16[4,2,128,128]{2,3,1,0:T(8,128)(2,1)S(1)} %fusion.20) | copy-start | bytes 786436
  41.9 21.7 %collective-permute-start.4 = (bf16[2,128,4,256]{1,3,2,0:T(8,128)(2,1)}, bf16[2,128,4,256]{1,3,2,0:T(8,128)(2,1)}, u32[]{:S(2)}, u32[]{:S(2)}) collective-permute-start(bf16[2,128,4,256]{1,3,2,0:T(8,128)(2,1)} %pad_maximum_fusion.1), channel_id=1, source_target_pairs={{8,0},{16,8},{24,16},{32,24},{40,32},{48,40},{56,48},{64,56},{72,6... | collective-permute-start | bytes 1572872 | tf_op jit(solution)/shard_map/ppermute | solution.py:19
  44.3 27.6 %collective-permute-start.5 = (bf16[2,128,4,256]{1,3,2,0:T(8,128)(2,1)}, bf16[2,128,4,256]{1,3,2,0:T(8,128)(2,1)}, u32[]{:S(2)}, u32[]{:S(2)}) collective-permute-start(bf16[2,128,4,256]{1,3,2,0:T(8,128)(2,1)} %pad_maximum_fusion.2), channel_id=1, source_target_pairs={{16,0},{24,8},{32,16},{40,24},{48,32},{56,40},{64,48},{72,56},{80,... | collective-permute-start | bytes 1572872 | tf_op jit(solution)/shard_map/ppermute | solution.py:19
  51.6 2.1 %copy-start.1 = (f32[1,128,2048]{2,1,0:T(8,128)S(1)}, f32[1,128,2048]{2,1,0:T(8,128)}, u32[]{:S(2)}) copy-start(f32[1,128,2048]{2,1,0:T(8,128)} %mul.242) | copy-start | bytes 3145732
  53.7 18.2 %copy-start.6 = (bf16[4,2,128,128]{2,3,1,0:T(8,128)(2,1)S(1)}, bf16[4,2,128,128]{2,3,1,0:T(8,128)(2,1)}, u32[]{:S(2)}) copy-start(bf16[4,2,128,128]{2,3,1,0:T(8,128)(2,1)} %copy-done.5) | copy-start | bytes 786436
  56.4 151.5 %copy-start.4 = (f32[4,2,128,128]{2,3,1,0:T(8,128)S(1)}, f32[4,2,128,128]{2,3,1,0:T(8,128)}, u32[]{:S(2)}) copy-start(f32[4,2,128,128]{2,3,1,0:T(8,128)} %copy-done.3) | copy-start | bytes 1572868
where the time goes:
time: 212 us; the launch traced here: 211 us
  blocking collectives  133 us (63%)
  local copies, waits for them, and re-layouts  20.3 us (10%)
  starting transfers between devices  20.1 us (9%)
  waiting for transfers between devices  15.5 us (7%)
  other arithmetic  11.1 us (5%)
  matrix products  9.73 us (5%)
    psum x1, blocking collectives, body(): q_total, k_total = lax.psum((q_sum_part, k_sum_part), ('ctx', 'dp'))  133 us
    ppermute x6, starting transfers between devices, shifted(): return lax.ppermute(value, axis, pairs)  20.1 us
    ppermute x6, waiting for transfers between devices, shifted(): return lax.ppermute(value, axis, pairs)  15.5 us
    unnamed x31, local copies, waits for them, and re-layouts  11 us
  transfers between devices with their start and end apart: 6, of which 2 were waited for; matrix products, arithmetic and copies ran while one was open for 13% of the time, Pallas kernels for 0%

commit v1 on v0

--- a/solution.py
+++ b/solution.py
@@ -1,3 +1,6 @@
+import itertools
+import math
+
 import jax
 import jax.numpy as jnp
 from jax import lax
@@ -11,6 +14,39 @@
 
 
 EPS = 1e-06
+
+
+RING_ORDER = {2: (0, 1), 4: (0, 1, 3, 2), 16: (11, 7, 12, 8, 15, 3, 0, 4, 9, 5, 10, 6, 13, 1, 14, 2)}
+AXIS_PARTS = {"ctx": (4, 16, 2), "dp": (4, 2)}
+
+
+def virtual_order(axis, count):
+    parts = AXIS_PARTS.get(axis)
+    if parts is None or count != math.prod(parts) or any(p not in RING_ORDER for p in parts):
+        return list(range(count))
+    order = []
+    for digits in itertools.product(*[range(p) for p in parts]):
+        index = 0
+        for digit, size in zip(digits, parts):
+            index = index * size + RING_ORDER[size][digit]
+        order.append(index)
+    return order
+
+
+def butterfly_sum(value):
+    for axis in ("dp", "ctx"):
+        count = lax.axis_size(axis)
+        if count & (count - 1):
+            value = lax.psum(value, axis)
+            continue
+        device_of = virtual_order(axis, count)
+        virtual_of = {device: virtual for virtual, device in enumerate(device_of)}
+        bit = 1
+        while bit < count:
+            pairs = [(device, device_of[virtual_of[device] ^ bit]) for device in range(count)]
+            value = value + lax.ppermute(value, axis, pairs)
+            bit *= 2
+    return value
 
 
 def shifted(value, axis, by):
@@ -150,7 +186,8 @@
     )
     q_sum_part = jnp.sum(q_grad_norm * q_normed, (0, 1))
     k_sum_part = jnp.sum(key_acc * normalized_keys, (0, 1))
-    q_total, k_total = lax.psum((q_sum_part, k_sum_part), ("ctx", "dp"))
+    gain_total = butterfly_sum(jnp.concatenate([q_sum_part, k_sum_part]))
+    q_total, k_total = gain_total[:HEAD_SIZE], gain_total[HEAD_SIZE:]
     factor = (lax.axis_size("ctx") * lax.axis_size("dp") * token_rows) ** (-0.5)
     return (
         attn_out.reshape(1, token_rows, QUERY_HEADS * HEAD_SIZE),

time: 212 us -> 157 us (0.74)
  the two profiles are of different devices: /device:TPU:1 before, /device:TPU:16 now
where the time goes in v1:
time: 157 us; the launch traced here: 156 us
  starting transfers between devices  69.1 us (44%)
  waiting for transfers between devices  52.8 us (34%)
  local copies, waits for them, and re-layouts  17.1 us (11%)
  matrix products  9.42 us (6%)
  other arithmetic  6.73 us (4%)
    ppermute x10, starting transfers between devices, butterfly_sum(): value = value + lax.ppermute(value, axis, pairs)  48.7 us
    ppermute x6, waiting for transfers between devices, shifted(): return lax.ppermute(value, axis, pairs)  30.6 us
    ppermute x10, waiting for transfers between devices, butterfly_sum(): value = value + lax.ppermute(value, axis, pairs)  22.2 us
    ppermute x6, starting transfers between devices, shifted(): return lax.ppermute(value, axis, pairs)  20.4 us
    unnamed x43, local copies, waits for them, and re-layouts  9.51 us
  transfers between devices with their start and end apart: 16, of which 12 were waited for; matrix products, arithmetic and copies ran while one was open for 15% of the time, Pallas kernels for 0%

profile of v1, /device:TPU:16, one launch (start us, length us, event | category | flops | bytes accessed | tf_op | source)
XLA Modules:
  0.0 156.4 jit_solution(9880995445157366057)
XLA Ops:
  1.3 4.3 %collective-permute-start.1 = (s32[128]{0:T(128)S(1)}, s32[128]{0:T(128)S(1)}, u32[]{:S(2)}, u32[]{:S(2)}) collective-permute-start(s32[128]{0:T(128)S(1)} %bitcast.294), channel_id=1, source_target_pairs={{0,16},{8,24},{16,32},{24,40},{32,48},{40,56},{48,64},{56,72},{64,... | collective-permute-start | bytes 1544 | tf_op jit(solution)/shard_map/ppermute | solution.py:55
  5.6 3.5 %collective-permute-start.2 = (s32[128]{0:T(128)S(1)}, s32[128]{0:T(128)S(1)}, u32[]{:S(2)}, u32[]{:S(2)}) collective-permute-start(s32[128]{0:T(128)S(1)} %bitcast.295), channel_id=1, source_target_pairs={{0,8},{8,16},{16,24},{24,32},{32,40},{40,48},{48,56},{56,64},{64,7... | collective-permute-start | bytes 1544 | tf_op jit(solution)/shard_map/ppermute | solution.py:55
  12.4 5.1 %collective-permute-start = (bf16[2,128,1024]{1,2,0:T(8,128)(2,1)}, bf16[2,128,1024]{1,2,0:T(8,128)(2,1)}, u32[]{:S(2)}, u32[]{:S(2)}) collective-permute-start(bf16[2,128,1024]{1,2,0:T(8,128)(2,1)} %pad_maximum_fusion), channel_id=1, source_target_pairs={{0,16},{8,24},{16,32},{24,40},{32,48},{40,56},{48,64},{56,72},{64,... | collective-permute-start | bytes 1572872 | tf_op jit(solution)/shard_map/ppermute | solution.py:55
  17.5 5.0 %collective-permute-start.3 = (bf16[2,128,1024]{1,2,0:T(8,128)(2,1)}, bf16[2,128,1024]{1,2,0:T(8,128)(2,1)}, u32[]{:S(2)}, u32[]{:S(2)}) collective-permute-start(bf16[2,128,1024]{1,2,0:T(8,128)(2,1)} %pad_maximum_fusion), channel_id=1, source_target_pairs={{0,8},{8,16},{16,24},{24,32},{32,40},{40,48},{48,56},{56,64},{64,7... | collective-permute-start | bytes 1572872 | tf_op jit(solution)/shard_map/ppermute | solution.py:55
  41.6 1.5 fusion.38
  43.0 19.5 %collective-permute-done.4 = bf16[2,128,4,256]{1,3,2,0:T(8,128)(2,1)S(1)} collective-permute-done((bf16[2,128,4,256]{1,3,2,0:T(8,128)(2,1)S(1)}, bf16[2,128,4,256]{1,3,2,0:T(8,128)(2,1)S(1)}, u32[]{:S(2)}, u32[]{:S(2)}) %collective-permute-start.4) | collective-permute-done | bytes 524320 | tf_op jit(solution)/shard_map/ppermute | solution.py:55
  62.5 9.8 %collective-permute-done.5 = bf16[2,128,4,256]{1,3,2,0:T(8,128)(2,1)S(1)} collective-permute-done((bf16[2,128,4,256]{1,3,2,0:T(8,128)(2,1)S(1)}, bf16[2,128,4,256]{1,3,2,0:T(8,128)(2,1)S(1)}, u32[]{:S(2)}, u32[]{:S(2)}) %collective-permute-start.5) | collective-permute-done | bytes 524320 | tf_op jit(solution)/shard_map/ppermute | solution.py:55
  73.5 1.9 %collective-permute-start.6 = (f32[512]{0:T(512)S(1)}, f32[512]{0:T(512)S(1)}, u32[]{:S(2)}, u32[]{:S(2)}) collective-permute-start(f32[512]{0:T(512)S(1)} %pad_maximum_fusion.3), channel_id=1, source_target_pairs={{0,1},{1,0},{2,3},{3,2},{4,5},{5,4},{6,7},{7,6},{8,9},{9,8},{10,11... | collective-permute-start | bytes 6152 | tf_op jit(solution)/shard_map/ppermute | solution.py:47
  76.6 2.2 %collective-permute-start.7 = (f32[512]{0:T(512)S(1)}, f32[512]{0:T(512)S(1)}, u32[]{:S(2)}, u32[]{:S(2)}) collective-permute-start(f32[512]{0:T(512)S(1)} %fusion.60), channel_id=1, source_target_pairs={{0,2},{1,3},{2,0},{3,1},{4,6},{5,7},{6,4},{7,5},{8,10},{9,11},{10,... | collective-permute-start | bytes 6152 | tf_op jit(solution)/shard_map/ppermute | solution.py:47
  78.8 4.1 %collective-permute-done.7 = f32[512]{0:T(512)S(1)} collective-permute-done((f32[512]{0:T(512)S(1)}, f32[512]{0:T(512)S(1)}, u32[]{:S(2)}, u32[]{:S(2)}) %collective-permute-start.7) | collective-permute-done | bytes 2080 | tf_op jit(solution)/shard_map/ppermute | solution.py:47
  82.9 5.7 %collective-permute-start.8 = (f32[512]{0:T(512)S(1)}, f32[512]{0:T(512)S(1)}, u32[]{:S(2)}, u32[]{:S(2)}) collective-permute-start(f32[512]{0:T(512)S(1)} %add.174), channel_id=1, source_target_pairs={{0,6},{1,7},{2,4},{3,5},{4,2},{5,3},{6,0},{7,1},{8,14},{9,15},{10,... | collective-permute-start | bytes 6152 | tf_op jit(solution)/shard_map/ppermute | solution.py:47
  88.6 1.9 %collective-permute-done.8 = f32[512]{0:T(512)S(1)} collective-permute-done((f32[512]{0:T(512)S(1)}, f32[512]{0:T(512)S(1)}, u32[]{:S(2)}, u32[]{:S(2)}) %collective-permute-start.8) | collective-permute-done | bytes 2080 | tf_op jit(solution)/shard_map/ppermute | solution.py:47
  90.5 1.9 %collective-permute-start.9 = (f32[512]{0:T(512)S(1)}, f32[512]{0:T(512)S(1)}, u32[]{:S(2)}, u32[]{:S(2)}) collective-permute-start(f32[512]{0:T(512)S(1)} %add.175), channel_id=1, source_target_pairs={{0,8},{8,0},{16,24},{24,16},{32,40},{40,32},{48,56},{56,48},{64,72... | collective-permute-start | bytes 6152 | tf_op jit(solution)/shard_map/ppermute | solution.py:47
  93.9 2.1 %collective-permute-done.9 = f32[512]{0:T(512)S(1)} collective-permute-done((f32[512]{0:T(512)S(1)}, f32[512]{0:T(512)S(1)}, u32[]{:S(2)}, u32[]{:S(2)}) %collective-permute-start.9) | collective-permute-done | bytes 2080 | tf_op jit(solution)/shard_map/ppermute | solution.py:47
  96.0 10.9 %collective-permute-start.10 = (f32[512]{0:T(512)S(1)}, f32[512]{0:T(512)S(1)}, u32[]{:S(2)}, u32[]{:S(2)}) collective-permute-start(f32[512]{0:T(512)S(1)} %add.176), channel_id=1, source_target_pairs={{0,64},{8,72},{16,208},{24,216},{32,224},{40,232},{48,240},{56,248... | collective-permute-start | bytes 6152 | tf_op jit(solution)/shard_map/ppermute | solution.py:47
  108.4 15.4 %collective-permute-start.11 = (f32[512]{0:T(512)S(1)}, f32[512]{0:T(512)S(1)}, u32[]{:S(2)}, u32[]{:S(2)}) collective-permute-start(f32[512]{0:T(512)S(1)} %add.177), channel_id=1, source_target_pairs={{0,240},{8,248},{16,32},{24,40},{32,16},{40,24},{48,64},{56,72},{6... | collective-permute-start | bytes 6152 | tf_op jit(solution)/shard_map/ppermute | solution.py:47
  126.6 1.9 %collective-permute-start.12 = (f32[512]{0:T(512)S(1)}, f32[512]{0:T(512)S(1)}, u32[]{:S(2)}, u32[]{:S(2)}) collective-permute-start(f32[512]{0:T(512)S(1)} %add.178), channel_id=1, source_target_pairs={{0,192},{8,200},{16,80},{24,88},{32,96},{40,104},{48,112},{56,120}... | collective-permute-start | bytes 6152 | tf_op jit(solution)/shard_map/ppermute | solution.py:47
  128.6 2.7 %multiply_convert_fusion = bf16[1,128,2048]{2,1,0:T(8,128)(2,1)} fusion(f32[1,128,2048]{2,1,0:T(8,128)S(1)} %copy-done.2, f32[1,128,2048]{2,1,0:T(8,128)} %mul.262, f32[1,128,2048]{2,1,0:T(8,128)} %copy.196, bf16[1,128,2048]{2,1,0:T(8,128)(2,1)S(1)} %copy-done, f32[2048]{0:T(1024)S(1)} %bitcast.276), kind=kLoop, calls=%fused_computation.56 | loop fusion | flops 1835008 | bytes 4202496 | tf_op jit(solution)/shard_map/convert_element_type | solution.py:176
  132.3 3.7 %collective-permute-done.12 = f32[512]{0:T(512)S(1)} collective-permute-done((f32[512]{0:T(512)S(1)}, f32[512]{0:T(512)S(1)}, u32[]{:S(2)}, u32[]{:S(2)}) %collective-permute-start.12) | collective-permute-done | bytes 2080 | tf_op jit(solution)/shard_map/ppermute | solution.py:47
  136.0 2.0 %collective-permute-start.13 = (f32[512]{0:T(512)S(1)}, f32[512]{0:T(512)S(1)}, u32[]{:S(2)}, u32[]{:S(2)}) collective-permute-start(f32[512]{0:T(512)S(1)} %add.179), channel_id=1, source_target_pairs={{0,224},{8,232},{16,48},{24,56},{32,64},{40,72},{48,16},{56,24},{6... | collective-permute-start | bytes 6152 | tf_op jit(solution)/shard_map/ppermute | solution.py:47
  139.4 4.3 %collective-permute-done.13 = f32[512]{0:T(512)S(1)} collective-permute-done((f32[512]{0:T(512)S(1)}, f32[512]{0:T(512)S(1)}, u32[]{:S(2)}, u32[]{:S(2)}) %collective-permute-start.13) | collective-permute-done | bytes 2080 | tf_op jit(solution)/shard_map/ppermute | solution.py:47
  143.7 3.3 %collective-permute-start.14 = (f32[512]{0:T(512)S(1)}, f32[512]{0:T(512)S(1)}, u32[]{:S(2)}, u32[]{:S(2)}) collective-permute-start(f32[512]{0:T(512)S(1)} %add.180), channel_id=1, source_target_pairs={{0,256},{8,264},{16,272},{24,280},{32,288},{40,296},{48,304},{56,3... | collective-permute-start | bytes 6152 | tf_op jit(solution)/shard_map/ppermute | solution.py:47
  147.1 2.1 %collective-permute-done.14 = f32[512]{0:T(512)S(1)} collective-permute-done((f32[512]{0:T(512)S(1)}, f32[512]{0:T(512)S(1)}, u32[]{:S(2)}, u32[]{:S(2)}) %collective-permute-start.14) | collective-permute-done | bytes 2080 | tf_op jit(solution)/shard_map/ppermute | solution.py:47
  149.2 3.4 %collective-permute-start.15 = (f32[512]{0:T(512)S(1)}, f32[512]{0:T(512)S(1)}, u32[]{:S(2)}, u32[]{:S(2)}) collective-permute-start(f32[512]{0:T(512)S(1)} %add.181), channel_id=1, source_target_pairs={{0,768},{8,776},{16,784},{24,792},{32,800},{40,808},{48,816},{56,8... | collective-permute-start | bytes 6152 | tf_op jit(solution)/shard_map/ppermute | solution.py:47
  (115 shorter events, 37.1 us)
Async XLA Ops:
  1.3 27.4 %collective-permute-start.1 = (s32[128]{0:T(128)S(1)}, s32[128]{0:T(128)S(1)}, u32[]{:S(2)}, u32[]{:S(2)}) collective-permute-start(s32[128]{0:T(128)S(1)} %bitcast.294), channel_id=1, source_target_pairs={{0,16},{8,24},{16,32},{24,40},{32,48},{40,56},{48,64},{56,72},{64,... | collective-permute-start | bytes 1544 | tf_op jit(solution)/shard_map/ppermute | solution.py:55
  5.6 23.2 %collective-permute-start.2 = (s32[128]{0:T(128)S(1)}, s32[128]{0:T(128)S(1)}, u32[]{:S(2)}, u32[]{:S(2)}) collective-permute-start(s32[128]{0:T(128)S(1)} %bitcast.295), channel_id=1, source_target_pairs={{0,8},{8,16},{16,24},{24,32},{32,40},{40,48},{48,56},{56,64},{64,7... | collective-permute-start | bytes 1544 | tf_op jit(solution)/shard_map/ppermute | solution.py:55
  11.5 10.9 %copy-start = (bf16[1,128,2048]{2,1,0:T(8,128)(2,1)S(1)}, bf16[1,128,2048]{2,1,0:T(8,128)(2,1)}, u32[]{:S(2)}) copy-start(bf16[1,128,2048]{2,1,0:T(8,128)(2,1)} %param.7) | copy-start | bytes 1572868
  12.4 17.0 %collective-permute-start = (bf16[2,128,1024]{1,2,0:T(8,128)(2,1)}, bf16[2,128,1024]{1,2,0:T(8,128)(2,1)}, u32[]{:S(2)}, u32[]{:S(2)}) collective-permute-start(bf16[2,128,1024]{1,2,0:T(8,128)(2,1)} %pad_maximum_fusion), channel_id=1, source_target_pairs={{0,16},{8,24},{16,32},{24,40},{32,48},{40,56},{48,64},{56,72},{64,... | collective-permute-start | bytes 1572872 | tf_op jit(solution)/shard_map/ppermute | solution.py:55
  17.5 14.8 %collective-permute-start.3 = (bf16[2,128,1024]{1,2,0:T(8,128)(2,1)}, bf16[2,128,1024]{1,2,0:T(8,128)(2,1)}, u32[]{:S(2)}, u32[]{:S(2)}) collective-permute-start(bf16[2,128,1024]{1,2,0:T(8,128)(2,1)} %pad_maximum_fusion), channel_id=1, source_target_pairs={{0,8},{8,16},{16,24},{24,32},{32,40},{40,48},{48,56},{56,64},{64,7... | collective-permute-start | bytes 1572872 | tf_op jit(solution)/shard_map/ppermute | solution.py:55
  28.7 8.6 %copy-start.3 = (bf16[1,128,2048]{1,2,0:T(8,128)(2,1)}, bf16[1,128,2048]{1,2,0:T(8,128)(2,1)S(1)}, u32[]{:S(2)}) copy-start(bf16[1,128,2048]{1,2,0:T(8,128)(2,1)S(1)} %copy.186) | copy-start | bytes 1572868
  29.4 8.0 %copy-start.7 = (f32[4,2,128,128]{2,3,1,0:T(8,128)}, f32[4,2,128,128]{2,3,1,0:T(8,128)S(1)}, u32[]{:S(2)}) copy-start(f32[4,2,128,128]{2,3,1,0:T(8,128)S(1)} %get-tuple-element.52) | copy-start | bytes 1572868
  38.0 24.5 %collective-permute-start.4 = (bf16[2,128,4,256]{1,3,2,0:T(8,128)(2,1)S(1)}, bf16[2,128,4,256]{1,3,2,0:T(8,128)(2,1)S(1)}, u32[]{:S(2)}, u32[]{:S(2)}) collective-permute-start(bf16[2,128,4,256]{1,3,2,0:T(8,128)(2,1)S(1)} %pad_maximum_fusion.1), channel_id=1, source_target_pairs={{8,0},{16,8},{24,16},{32,24},{40,32},{48,40},{56,48},{64,56},{72,6... | collective-permute-start | bytes 1572872 | tf_op jit(solution)/shard_map/ppermute | solution.py:55
  39.6 32.7 %collective-permute-start.5 = (bf16[2,128,4,256]{1,3,2,0:T(8,128)(2,1)S(1)}, bf16[2,128,4,256]{1,3,2,0:T(8,128)(2,1)S(1)}, u32[]{:S(2)}, u32[]{:S(2)}) collective-permute-start(bf16[2,128,4,256]{1,3,2,0:T(8,128)(2,1)S(1)} %pad_maximum_fusion.2), channel_id=1, source_target_pairs={{16,0},{24,8},{32,16},{40,24},{48,32},{56,40},{64,48},{72,56},{80,... | collective-permute-start | bytes 1572872 | tf_op jit(solution)/shard_map/ppermute | solution.py:55
  62.5 11.0 %copy-start.14 = (bf16[2,128,4,256]{1,3,2,0:T(8,128)(2,1)}, bf16[2,128,4,256]{1,3,2,0:T(8,128)(2,1)S(1)}, u32[]{:S(2)}) copy-start(bf16[2,128,4,256]{1,3,2,0:T(8,128)(2,1)S(1)} %collective-permute-done.4) | copy-start | bytes 1572868
  73.5 3.1 %collective-permute-start.6 = (f32[512]{0:T(512)S(1)}, f32[512]{0:T(512)S(1)}, u32[]{:S(2)}, u32[]{:S(2)}) collective-permute-start(f32[512]{0:T(512)S(1)} %pad_maximum_fusion.3), channel_id=1, source_target_pairs={{0,1},{1,0},{2,3},{3,2},{4,5},{5,4},{6,7},{7,6},{8,9},{9,8},{10,11... | collective-permute-start | bytes 6152 | tf_op jit(solution)/shard_map/ppermute | solution.py:47
  76.6 6.4 %collective-permute-start.7 = (f32[512]{0:T(512)S(1)}, f32[512]{0:T(512)S(1)}, u32[]{:S(2)}, u32[]{:S(2)}) collective-permute-start(f32[512]{0:T(512)S(1)} %fusion.60), channel_id=1, source_target_pairs={{0,2},{1,3},{2,0},{3,1},{4,6},{5,7},{6,4},{7,5},{8,10},{9,11},{10,... | collective-permute-start | bytes 6152 | tf_op jit(solution)/shard_map/ppermute | solution.py:47
  82.9 7.6 %collective-permute-start.8 = (f32[512]{0:T(512)S(1)}, f32[512]{0:T(512)S(1)}, u32[]{:S(2)}, u32[]{:S(2)}) collective-permute-start(f32[512]{0:T(512)S(1)} %add.174), channel_id=1, source_target_pairs={{0,6},{1,7},{2,4},{3,5},{4,2},{5,3},{6,0},{7,1},{8,14},{9,15},{10,... | collective-permute-start | bytes 6152 | tf_op jit(solution)/shard_map/ppermute | solution.py:47
  90.5 5.5 %collective-permute-start.9 = (f32[512]{0:T(512)S(1)}, f32[512]{0:T(512)S(1)}, u32[]{:S(2)}, u32[]{:S(2)}) collective-permute-start(f32[512]{0:T(512)S(1)} %add.175), channel_id=1, source_target_pairs={{0,8},{8,0},{16,24},{24,16},{32,40},{40,32},{48,56},{56,48},{64,72... | collective-permute-start | bytes 6152 | tf_op jit(solution)/shard_map/ppermute | solution.py:47
  92.7 14.1 %copy-start.1 = (f32[4,256,2,128]{3,1,2,0:T(8,128)S(1)}, f32[4,256,2,128]{3,1,2,0:T(8,128)}, u32[]{:S(2)}) copy-start(f32[4,256,2,128]{3,1,2,0:T(8,128)} %get-tuple-element.59) | copy-start | bytes 3145732
  96.0 12.5 %collective-permute-start.10 = (f32[512]{0:T(512)S(1)}, f32[512]{0:T(512)S(1)}, u32[]{:S(2)}, u32[]{:S(2)}) collective-permute-start(f32[512]{0:T(512)S(1)} %add.176), channel_id=1, source_target_pairs={{0,64},{8,72},{16,208},{24,216},{32,224},{40,232},{48,240},{56,248... | collective-permute-start | bytes 6152 | tf_op jit(solution)/shard_map/ppermute | solution.py:47
  108.4 18.2 %collective-permute-start.11 = (f32[512]{0:T(512)S(1)}, f32[512]{0:T(512)S(1)}, u32[]{:S(2)}, u32[]{:S(2)}) collective-permute-start(f32[512]{0:T(512)S(1)} %add.177), channel_id=1, source_target_pairs={{0,240},{8,248},{16,32},{24,40},{32,16},{40,24},{48,64},{56,72},{6... | collective-permute-start | bytes 6152 | tf_op jit(solution)/shard_map/ppermute | solution.py:47
  126.6 9.4 %collective-permute-start.12 = (f32[512]{0:T(512)S(1)}, f32[512]{0:T(512)S(1)}, u32[]{:S(2)}, u32[]{:S(2)}) collective-permute-start(f32[512]{0:T(512)S(1)} %add.178), channel_id=1, source_target_pairs={{0,192},{8,200},{16,80},{24,88},{32,96},{40,104},{48,112},{56,120}... | collective-permute-start | bytes 6152 | tf_op jit(solution)/shard_map/ppermute | solution.py:47
  131.3 6.8 %copy-start.4 = (bf16[1,128,2048]{1,2,0:T(8,128)(2,1)S(1)}, bf16[1,128,2048]{1,2,0:T(8,128)(2,1)}, u32[]{:S(2)}) copy-start(bf16[1,128,2048]{1,2,0:T(8,128)(2,1)} %copy-done.3) | copy-start | bytes 1572868
  131.3 6.8 %copy-start.8 = (f32[4,2,128,128]{2,3,1,0:T(8,128)S(1)}, f32[4,2,128,128]{2,3,1,0:T(8,128)}, u32[]{:S(2)}) copy-start(f32[4,2,128,128]{2,3,1,0:T(8,128)} %copy-done.7) | copy-start | bytes 1572868
  136.0 16.6 %copy-start.9 = (f32[128,4,256]{0,2,1:T(8,128)S(1)}, f32[128,4,256]{0,2,1:T(8,128)}, u32[]{:S(2)}) copy-start(f32[128,4,256]{0,2,1:T(8,128)} %get-tuple-element.60) | copy-start | bytes 1572868
  136.0 7.7 %collective-permute-start.13 = (f32[512]{0:T(512)S(1)}, f32[512]{0:T(512)S(1)}, u32[]{:S(2)}, u32[]{:S(2)}) collective-permute-start(f32[512]{0:T(512)S(1)} %add.179), channel_id=1, source_target_pairs={{0,224},{8,232},{16,48},{24,56},{32,64},{40,72},{48,16},{56,24},{6... | collective-permute-start | bytes 6152 | tf_op jit(solution)/shard_map/ppermute | solution.py:47
  143.7 5.5 %collective-permute-start.14 = (f32[512]{0:T(512)S(1)}, f32[512]{0:T(512)S(1)}, u32[]{:S(2)}, u32[]{:S(2)}) collective-permute-start(f32[512]{0:T(512)S(1)} %add.180), channel_id=1, source_target_pairs={{0,256},{8,264},{16,272},{24,280},{32,288},{40,296},{48,304},{56,3... | collective-permute-start | bytes 6152 | tf_op jit(solution)/shard_map/ppermute | solution.py:47
  149.2 6.7 %collective-permute-start.15 = (f32[512]{0:T(512)S(1)}, f32[512]{0:T(512)S(1)}, u32[]{:S(2)}, u32[]{:S(2)}) collective-permute-start(f32[512]{0:T(512)S(1)} %add.181), channel_id=1, source_target_pairs={{0,768},{8,776},{16,784},{24,792},{32,800},{40,808},{48,816},{56,8... | collective-permute-start | bytes 6152 | tf_op jit(solution)/shard_map/ppermute | solution.py:47
  (8 other events, 11.0 us)

commit v2 on v1

--- a/solution.py
+++ b/solution.py
@@ -14,6 +14,7 @@
 
 
 EPS = 1e-06
+GAIN_ROUNDS_BEFORE_RETURN = 5
 
 
 RING_ORDER = {2: (0, 1), 4: (0, 1, 3, 2), 16: (11, 7, 12, 8, 15, 3, 0, 4, 9, 5, 10, 6, 13, 1, 14, 2)}
@@ -33,19 +34,29 @@
     return order
 
 
-def butterfly_sum(value):
+def butterfly_rounds():
+    rounds = []
     for axis in ("dp", "ctx"):
         count = lax.axis_size(axis)
         if count & (count - 1):
-            value = lax.psum(value, axis)
+            rounds.append((axis, None))
             continue
         device_of = virtual_order(axis, count)
         virtual_of = {device: virtual for virtual, device in enumerate(device_of)}
         bit = 1
         while bit < count:
             pairs = [(device, device_of[virtual_of[device] ^ bit]) for device in range(count)]
+            rounds.append((axis, pairs))
+            bit *= 2
+    return rounds
+
+
+def apply_rounds(value, rounds):
+    for axis, pairs in rounds:
+        if pairs is None:
+            value = lax.psum(value, axis)
+        else:
             value = value + lax.ppermute(value, axis, pairs)
-            bit *= 2
     return value
 
 
@@ -77,9 +88,7 @@
         keys[0], KEY_VALUE_HEADS, key_norm_gain
     )
     own_seg = segment_ids[0]
-    local_key_value = jnp.stack(
-        [key_norm_result.reshape(token_rows, KEY_VALUE_HEADS * HEAD_SIZE), values[0]]
-    )
+    local_key_value = jnp.stack([keys[0], values[0]])
     received = []
     for offset in range(1, HALO + 1):
         received.append(shifted((local_key_value, own_seg), "ctx", offset))
@@ -90,8 +99,16 @@
         token_rows, KEY_VALUE_HEADS, query_group_width, HEAD_SIZE
     )
     key_block_list, value_block_list, key_masks, live_flags = ([], [], [], [])
+    key_hat_list = []
     for block in range(HALO + 1):
         key_value_pair, seg_block = blocks[block]
+        if block == HALO:
+            block_hat, block_norm = normalized_keys, key_norm_result
+        else:
+            block_hat, _, block_norm = rms_normalize(
+                key_value_pair[0], KEY_VALUE_HEADS, key_norm_gain
+            )
+        key_hat_list.append(block_hat)
         k_pos = (ctx_index - HALO + block) * token_rows + positions
         distance = q_pos[:, None] - k_pos[None, :]
         key_mask = (
@@ -100,7 +117,7 @@
             & (k_pos[None, :] >= 0)
             & (own_seg[:, None] == seg_block[None, :])
         )
-        key_block_list.append(key_value_pair[0].reshape(token_rows, KEY_VALUE_HEADS, HEAD_SIZE))
+        key_block_list.append(block_norm)
         value_block_list.append(key_value_pair[1].reshape(token_rows, KEY_VALUE_HEADS, HEAD_SIZE))
         key_masks.append(key_mask)
         live_flags.append(jnp.any(key_mask))
@@ -162,13 +179,24 @@
     q_grad_norm = (sum((item[0] for item in back_blocks)) * score_scale).reshape(
         token_rows, QUERY_HEADS, HEAD_SIZE
     )
+    q_sum_part = jnp.sum(q_grad_norm * q_normed, (0, 1))
+    k_sum_part = sum(
+        jnp.sum(back_blocks[block][1].astype(jnp.float32) * key_hat_list[block], (0, 1))
+        for block in range(HALO + 1)
+    )
+    rounds = butterfly_rounds()
+    split = min(GAIN_ROUNDS_BEFORE_RETURN, len(rounds))
+    gain_partial = apply_rounds(jnp.concatenate([q_sum_part, k_sum_part]), rounds[:split])
+    returned_list = [
+        shifted(jnp.stack([back_blocks[HALO - offset][1], back_blocks[HALO - offset][2]]), "ctx", -offset)
+        for offset in range(1, HALO + 1)
+    ]
+    returned_list, gain_partial = lax.optimization_barrier((returned_list, gain_partial))
+    gain_total = apply_rounds(gain_partial, rounds[split:])
+    q_total, k_total = gain_total[:HEAD_SIZE], gain_total[HEAD_SIZE:]
     key_acc = back_blocks[HALO][1].astype(jnp.float32)
     value_accumulator = back_blocks[HALO][2].astype(jnp.float32)
-    for offset in range(1, HALO + 1):
-        block = HALO - offset
-        returned = shifted(
-            jnp.stack([back_blocks[block][1], back_blocks[block][2]]), "ctx", -offset
-        )
+    for returned in returned_list:
         key_acc = key_acc + returned[0].astype(jnp.float32)
         value_accumulator = value_accumulator + returned[1].astype(jnp.float32)
     grad_queries = (
@@ -184,10 +212,6 @@
     value_gradient = value_accumulator.astype(jnp.bfloat16).reshape(
         1, token_rows, KEY_VALUE_HEADS * HEAD_SIZE
     )
-    q_sum_part = jnp.sum(q_grad_norm * q_normed, (0, 1))
-    k_sum_part = jnp.sum(key_acc * normalized_keys, (0, 1))
-    gain_total = butterfly_sum(jnp.concatenate([q_sum_part, k_sum_part]))
-    q_total, k_total = gain_total[:HEAD_SIZE], gain_total[HEAD_SIZE:]
     factor = (lax.axis_size("ctx") * lax.axis_size("dp") * token_rows) ** (-0.5)
     return (
         attn_out.reshape(1, token_rows, QUERY_HEADS * HEAD_SIZE),

time: 157 us -> 148 us (0.943)
  the two profiles are of different devices: /device:TPU:16 before, /device:TPU:24 now
where the time goes in v2:
time: 148 us; the launch traced here: 147 us
  starting transfers between devices  73.9 us (50%)
  waiting for transfers between devices  28.2 us (19%)
  local copies, waits for them, and re-layouts  22 us (15%)
  other arithmetic  13.1 us (9%)
  matrix products  8.88 us (6%)
    ppermute x10, starting transfers between devices, apply_rounds(): value = value + lax.ppermute(value, axis, pairs)  54.4 us
    ppermute x10, waiting for transfers between devices, apply_rounds(): value = value + lax.ppermute(value, axis, pairs)  20 us
    ppermute x6, starting transfers between devices, shifted(): return lax.ppermute(value, axis, pairs)  19.5 us
    unnamed x40, local copies, waits for them, and re-layouts  11.7 us
    ppermute x6, waiting for transfers between devices, shifted(): return lax.ppermute(value, axis, pairs)  8.19 us
    convert_element_type x1, other arithmetic, body(): grad_queries = rms_norm_backward(q_grad_norm, q_normed, q_inv, q_gain).as...  3.02 us
  transfers between devices with their start and end apart: 16, of which 7 were waited for; matrix products, arithmetic and copies ran while one was open for 18% of the time, Pallas kernels for 0%

profile of v2, /device:TPU:24, one launch (start us, length us, event | category | flops | bytes accessed | tf_op | source)
XLA Modules:
  0.0 147.2 jit_solution(11060016900620847324)
XLA Ops:
  1.3 4.4 %collective-permute-start.1 = (s32[128]{0:T(128)S(1)}, s32[128]{0:T(128)S(1)}, u32[]{:S(2)}, u32[]{:S(2)}) collective-permute-start(s32[128]{0:T(128)S(1)} %bitcast.295), channel_id=1, source_target_pairs={{0,16},{8,24},{16,32},{24,40},{32,48},{40,56},{48,64},{56,72},{64,... | collective-permute-start | bytes 1544 | tf_op jit(solution)/shard_map/ppermute | solution.py:66
  5.7 4.2 %collective-permute-start.2 = (s32[128]{0:T(128)S(1)}, s32[128]{0:T(128)S(1)}, u32[]{:S(2)}, u32[]{:S(2)}) collective-permute-start(s32[128]{0:T(128)S(1)} %bitcast.296), channel_id=1, source_target_pairs={{0,8},{8,16},{16,24},{24,32},{32,40},{40,48},{48,56},{56,64},{64,7... | collective-permute-start | bytes 1544 | tf_op jit(solution)/shard_map/ppermute | solution.py:66
  9.9 1.7 %constant_dynamic-update-slice_fusion.1 = bf16[2,128,1024]{2,1,0:T(8,128)(2,1)} fusion(bf16[1,128,1024]{2,1,0:T(8,128)(2,1)} %param.8), kind=kLoop, calls=%fused_computation.109 | loop fusion | bytes 524288
  12.3 5.1 %collective-permute-start = (bf16[2,128,1024]{2,1,0:T(8,128)(2,1)}, bf16[2,128,1024]{2,1,0:T(8,128)(2,1)}, u32[]{:S(2)}, u32[]{:S(2)}) collective-permute-start(bf16[2,128,1024]{2,1,0:T(8,128)(2,1)} %constant_dynamic-update-slice_fusion), channel_id=1, source_target_pairs={{0,16},{8,24},{16,32},{24,40},{32,48},{40,56},{48,64},{56,72},{64,... | collective-permute-start | bytes 1572872 | tf_op jit(solution)/shard_map/ppermute | solution.py:66
  17.3 2.7 %collective-permute-start.3 = (bf16[2,128,1024]{2,1,0:T(8,128)(2,1)}, bf16[2,128,1024]{2,1,0:T(8,128)(2,1)}, u32[]{:S(2)}, u32[]{:S(2)}) collective-permute-start(bf16[2,128,1024]{2,1,0:T(8,128)(2,1)} %constant_dynamic-update-slice_fusion), channel_id=1, source_target_pairs={{0,8},{8,16},{16,24},{24,32},{32,40},{40,48},{48,56},{56,64},{64,7... | collective-permute-start | bytes 1572872 | tf_op jit(solution)/shard_map/ppermute | solution.py:66
  30.5 8.2 %collective-permute-done.3 = bf16[2,128,1024]{2,1,0:T(8,128)(2,1)} collective-permute-done((bf16[2,128,1024]{2,1,0:T(8,128)(2,1)}, bf16[2,128,1024]{2,1,0:T(8,128)(2,1)}, u32[]{:S(2)}, u32[]{:S(2)}) %collective-permute-start.3) | collective-permute-done | bytes 524320 | tf_op jit(solution)/shard_map/ppermute | solution.py:66
  38.7 2.0 %slice_convert_fusion = (f32[1,128,1024]{2,1,0:T(8,128)}, bf16[1,128,1024]{2,1,0:T(8,128)(2,1)}) fusion(bf16[2,128,1024]{2,1,0:T(8,128)(2,1)} %collective-permute-done.3), kind=kLoop, calls=%fused_computation.85 | loop fusion | flops 131072 | bytes 1310720 | tf_op jit(solution)/shard_map/convert_element_type | solution.py:70
  42.0 1.8 %copy.201 = bf16[1,128,1024]{1,2,0:T(8,128)(2,1)} copy(bf16[1,128,1024]{2,1,0:T(8,128)(2,1)} %get-tuple-element.47) | data formatting | bytes 524288 | tf_op jit(solution)/shard_map/slice | solution.py:121
  53.2 1.9 %collective-permute-start.6 = (f32[512]{0:T(512)S(1)}, f32[512]{0:T(512)S(1)}, u32[]{:S(2)}, u32[]{:S(2)}) collective-permute-start(f32[512]{0:T(512)S(1)} %pad_maximum_fusion.2), channel_id=1, source_target_pairs={{0,1},{1,0},{2,3},{3,2},{4,5},{5,4},{6,7},{7,6},{8,9},{9,8},{10,11... | collective-permute-start | bytes 6152 | tf_op jit(solution)/shard_map/ppermute | solution.py:59
  57.3 2.3 %collective-permute-start.7 = (f32[512]{0:T(512)S(1)}, f32[512]{0:T(512)S(1)}, u32[]{:S(2)}, u32[]{:S(2)}) collective-permute-start(f32[512]{0:T(512)S(1)} %fusion.64), channel_id=1, source_target_pairs={{0,2},{1,3},{2,0},{3,1},{4,6},{5,7},{6,4},{7,5},{8,10},{9,11},{10,... | collective-permute-start | bytes 6152 | tf_op jit(solution)/shard_map/ppermute | solution.py:59
  60.4 1.9 %collective-permute-start.4 = (bf16[2,128,4,256]{1,3,2,0:T(8,128)(2,1)}, bf16[2,128,4,256]{1,3,2,0:T(8,128)(2,1)}, u32[]{:S(2)}, u32[]{:S(2)}) collective-permute-start(bf16[2,128,4,256]{1,3,2,0:T(8,128)(2,1)} %pad_maximum_fusion), channel_id=1, source_target_pairs={{8,0},{16,8},{24,16},{32,24},{40,32},{48,40},{56,48},{64,56},{72,6... | collective-permute-start | bytes 1572872 | tf_op jit(solution)/shard_map/ppermute | solution.py:66
  63.7 5.7 %collective-permute-start.8 = (f32[512]{0:T(512)S(1)}, f32[512]{0:T(512)S(1)}, u32[]{:S(2)}, u32[]{:S(2)}) collective-permute-start(f32[512]{0:T(512)S(1)} %add.192), channel_id=1, source_target_pairs={{0,6},{1,7},{2,4},{3,5},{4,2},{5,3},{6,0},{7,1},{8,14},{9,15},{10,... | collective-permute-start | bytes 6152 | tf_op jit(solution)/shard_map/ppermute | solution.py:59
  70.9 8.3 %collective-permute-done.8 = f32[512]{0:T(512)S(1)} collective-permute-done((f32[512]{0:T(512)S(1)}, f32[512]{0:T(512)S(1)}, u32[]{:S(2)}, u32[]{:S(2)}) %collective-permute-start.8) | collective-permute-done | bytes 2080 | tf_op jit(solution)/shard_map/ppermute | solution.py:59
  79.1 1.9 %collective-permute-start.9 = (f32[512]{0:T(512)S(1)}, f32[512]{0:T(512)S(1)}, u32[]{:S(2)}, u32[]{:S(2)}) collective-permute-start(f32[512]{0:T(512)S(1)} %add.193), channel_id=1, source_target_pairs={{0,8},{8,0},{16,24},{24,16},{32,40},{40,32},{48,56},{56,48},{64,72... | collective-permute-start | bytes 6152 | tf_op jit(solution)/shard_map/ppermute | solution.py:59
  81.2 3.6 %collective-permute-done.9 = f32[512]{0:T(512)S(1)} collective-permute-done((f32[512]{0:T(512)S(1)}, f32[512]{0:T(512)S(1)}, u32[]{:S(2)}, u32[]{:S(2)}) %collective-permute-start.9) | collective-permute-done | bytes 2080 | tf_op jit(solution)/shard_map/ppermute | solution.py:59
  84.8 13.9 %collective-permute-start.10 = (f32[512]{0:T(512)S(1)}, f32[512]{0:T(512)S(1)}, u32[]{:S(2)}, u32[]{:S(2)}) collective-permute-start(f32[512]{0:T(512)S(1)} %add.194), channel_id=1, source_target_pairs={{0,64},{8,72},{16,208},{24,216},{32,224},{40,232},{48,240},{56,248... | collective-permute-start | bytes 6152 | tf_op jit(solution)/shard_map/ppermute | solution.py:59
  101.5 9.9 %collective-permute-start.11 = (f32[512]{0:T(512)S(1)}, f32[512]{0:T(512)S(1)}, u32[]{:S(2)}, u32[]{:S(2)}) collective-permute-start(f32[512]{0:T(512)S(1)} %add.195), channel_id=1, source_target_pairs={{0,240},{8,248},{16,32},{24,40},{32,16},{40,24},{48,64},{56,72},{6... | collective-permute-start | bytes 6152 | tf_op jit(solution)/shard_map/ppermute | solution.py:59
  111.5 3.0 %multiply_convert_fusion = bf16[1,128,2048]{2,1,0:T(8,128)(2,1)} fusion(f32[1,128,2048]{2,1,0:T(8,128)} %mul.278, f32[1,128,2048]{2,1,0:T(8,128)} %mul.298, f32[1,128,2048]{2,1,0:T(8,128)} %copy.217, bf16[1,128,2048]{2,1,0:T(8,128)(2,1)S(1)} %copy-done.1, f32[2048]{0:T(1024)S(1)} %bitcast.281), kind=kLoop, calls=%fused_computation.57 | loop fusion | flops 1835008 | bytes 4202496 | tf_op jit(solution)/shard_map/convert_element_type | solution.py:204
  115.5 5.0 %collective-permute-start.12 = (f32[512]{0:T(512)S(1)}, f32[512]{0:T(512)S(1)}, u32[]{:S(2)}, u32[]{:S(2)}) collective-permute-start(f32[512]{0:T(512)S(1)} %add.200), channel_id=1, source_target_pairs={{0,192},{8,200},{16,80},{24,88},{32,96},{40,104},{48,112},{56,120}... | collective-permute-start | bytes 6152 | tf_op jit(solution)/shard_map/ppermute | solution.py:59
  121.7 3.2 %collective-permute-done.12 = f32[512]{0:T(512)S(1)} collective-permute-done((f32[512]{0:T(512)S(1)}, f32[512]{0:T(512)S(1)}, u32[]{:S(2)}, u32[]{:S(2)}) %collective-permute-start.12) | collective-permute-done | bytes 2080 | tf_op jit(solution)/shard_map/ppermute | solution.py:59
  124.9 4.8 %collective-permute-start.13 = (f32[512]{0:T(512)S(1)}, f32[512]{0:T(512)S(1)}, u32[]{:S(2)}, u32[]{:S(2)}) collective-permute-start(f32[512]{0:T(512)S(1)} %add.201), channel_id=1, source_target_pairs={{0,224},{8,232},{16,48},{24,56},{32,64},{40,72},{48,16},{56,24},{6... | collective-permute-start | bytes 6152 | tf_op jit(solution)/shard_map/ppermute | solution.py:59
  129.7 2.7 %collective-permute-done.13 = f32[512]{0:T(512)S(1)} collective-permute-done((f32[512]{0:T(512)S(1)}, f32[512]{0:T(512)S(1)}, u32[]{:S(2)}, u32[]{:S(2)}) %collective-permute-start.13) | collective-permute-done | bytes 2080 | tf_op jit(solution)/shard_map/ppermute | solution.py:59
  132.5 3.5 %collective-permute-start.14 = (f32[512]{0:T(512)S(1)}, f32[512]{0:T(512)S(1)}, u32[]{:S(2)}, u32[]{:S(2)}) collective-permute-start(f32[512]{0:T(512)S(1)} %add.202), channel_id=1, source_target_pairs={{0,256},{8,264},{16,272},{24,280},{32,288},{40,296},{48,304},{56,3... | collective-permute-start | bytes 6152 | tf_op jit(solution)/shard_map/ppermute | solution.py:59
  138.1 5.5 %collective-permute-start.15 = (f32[512]{0:T(512)S(1)}, f32[512]{0:T(512)S(1)}, u32[]{:S(2)}, u32[]{:S(2)}) collective-permute-start(f32[512]{0:T(512)S(1)} %add.203), channel_id=1, source_target_pairs={{0,768},{8,776},{16,784},{24,792},{32,800},{40,808},{48,816},{56,8... | collective-permute-start | bytes 6152 | tf_op jit(solution)/shard_map/ppermute | solution.py:59
  (122 shorter events, 38.9 us)
Async XLA Ops:
  0.6 10.9 %copy-start.3 = (bf16[1,128,1024]{2,1,0:T(8,128)(2,1)S(1)}, bf16[1,128,1024]{2,1,0:T(8,128)(2,1)}, u32[]{:S(2)}) copy-start(bf16[1,128,1024]{2,1,0:T(8,128)(2,1)} %param.9) | copy-start | bytes 786436
  1.3 18.8 %copy-start = (bf16[1,128,2048]{2,1,0:T(8,128)(2,1)S(1)}, bf16[1,128,2048]{2,1,0:T(8,128)(2,1)}, u32[]{:S(2)}) copy-start(bf16[1,128,2048]{2,1,0:T(8,128)(2,1)} %param.7) | copy-start | bytes 1572868
  1.3 25.8 %collective-permute-start.1 = (s32[128]{0:T(128)S(1)}, s32[128]{0:T(128)S(1)}, u32[]{:S(2)}, u32[]{:S(2)}) collective-permute-start(s32[128]{0:T(128)S(1)} %bitcast.295), channel_id=1, source_target_pairs={{0,16},{8,24},{16,32},{24,40},{32,48},{40,56},{48,64},{56,72},{64,... | collective-permute-start | bytes 1544 | tf_op jit(solution)/shard_map/ppermute | solution.py:66
  5.7 21.4 %collective-permute-start.2 = (s32[128]{0:T(128)S(1)}, s32[128]{0:T(128)S(1)}, u32[]{:S(2)}, u32[]{:S(2)}) collective-permute-start(s32[128]{0:T(128)S(1)} %bitcast.296), channel_id=1, source_target_pairs={{0,8},{8,16},{16,24},{24,32},{32,40},{40,48},{48,56},{56,64},{64,7... | collective-permute-start | bytes 1544 | tf_op jit(solution)/shard_map/ppermute | solution.py:66
  12.3 16.9 %collective-permute-start = (bf16[2,128,1024]{2,1,0:T(8,128)(2,1)}, bf16[2,128,1024]{2,1,0:T(8,128)(2,1)}, u32[]{:S(2)}, u32[]{:S(2)}) collective-permute-start(bf16[2,128,1024]{2,1,0:T(8,128)(2,1)} %constant_dynamic-update-slice_fusion), channel_id=1, source_target_pairs={{0,16},{8,24},{16,32},{24,40},{32,48},{40,56},{48,64},{56,72},{64,... | collective-permute-start | bytes 1572872 | tf_op jit(solution)/shard_map/ppermute | solution.py:66
  17.3 21.4 %collective-permute-start.3 = (bf16[2,128,1024]{2,1,0:T(8,128)(2,1)}, bf16[2,128,1024]{2,1,0:T(8,128)(2,1)}, u32[]{:S(2)}, u32[]{:S(2)}) collective-permute-start(bf16[2,128,1024]{2,1,0:T(8,128)(2,1)} %constant_dynamic-update-slice_fusion), channel_id=1, source_target_pairs={{0,8},{8,16},{16,24},{24,32},{32,40},{40,48},{48,56},{56,64},{64,7... | collective-permute-start | bytes 1572872 | tf_op jit(solution)/shard_map/ppermute | solution.py:66
  46.9 1.2 copy-start.8
  46.9 1.3 copy-start.11
  53.2 4.1 %collective-permute-start.6 = (f32[512]{0:T(512)S(1)}, f32[512]{0:T(512)S(1)}, u32[]{:S(2)}, u32[]{:S(2)}) collective-permute-start(f32[512]{0:T(512)S(1)} %pad_maximum_fusion.2), channel_id=1, source_target_pairs={{0,1},{1,0},{2,3},{3,2},{4,5},{5,4},{6,7},{7,6},{8,9},{9,8},{10,11... | collective-permute-start | bytes 6152 | tf_op jit(solution)/shard_map/ppermute | solution.py:59
  56.0 45.5 %collective-permute-start.5 = (bf16[2,128,4,256]{1,3,2,0:T(8,128)(2,1)}, bf16[2,128,4,256]{1,3,2,0:T(8,128)(2,1)}, u32[]{:S(2)}, u32[]{:S(2)}) collective-permute-start(bf16[2,128,4,256]{1,3,2,0:T(8,128)(2,1)} %pad_maximum_fusion.1), channel_id=1, source_target_pairs={{16,0},{24,8},{32,16},{40,24},{48,32},{56,40},{64,48},{72,56},{80,... | collective-permute-start | bytes 1572872 | tf_op jit(solution)/shard_map/ppermute | solution.py:66
  57.3 6.4 %collective-permute-start.7 = (f32[512]{0:T(512)S(1)}, f32[512]{0:T(512)S(1)}, u32[]{:S(2)}, u32[]{:S(2)}) collective-permute-start(f32[512]{0:T(512)S(1)} %fusion.64), channel_id=1, source_target_pairs={{0,2},{1,3},{2,0},{3,1},{4,6},{5,7},{6,4},{7,5},{8,10},{9,11},{10,... | collective-permute-start | bytes 6152 | tf_op jit(solution)/shard_map/ppermute | solution.py:59
  60.4 41.0 %collective-permute-start.4 = (bf16[2,128,4,256]{1,3,2,0:T(8,128)(2,1)}, bf16[2,128,4,256]{1,3,2,0:T(8,128)(2,1)}, u32[]{:S(2)}, u32[]{:S(2)}) collective-permute-start(bf16[2,128,4,256]{1,3,2,0:T(8,128)(2,1)} %pad_maximum_fusion), channel_id=1, source_target_pairs={{8,0},{16,8},{24,16},{32,24},{40,32},{48,40},{56,48},{64,56},{72,6... | collective-permute-start | bytes 1572872 | tf_op jit(solution)/shard_map/ppermute | solution.py:66
  63.7 15.4 %collective-permute-start.8 = (f32[512]{0:T(512)S(1)}, f32[512]{0:T(512)S(1)}, u32[]{:S(2)}, u32[]{:S(2)}) collective-permute-start(f32[512]{0:T(512)S(1)} %add.192), channel_id=1, source_target_pairs={{0,6},{1,7},{2,4},{3,5},{4,2},{5,3},{6,0},{7,1},{8,14},{9,15},{10,... | collective-permute-start | bytes 6152 | tf_op jit(solution)/shard_map/ppermute | solution.py:59
  79.1 5.6 %collective-permute-start.9 = (f32[512]{0:T(512)S(1)}, f32[512]{0:T(512)S(1)}, u32[]{:S(2)}, u32[]{:S(2)}) collective-permute-start(f32[512]{0:T(512)S(1)} %add.193), channel_id=1, source_target_pairs={{0,8},{8,0},{16,24},{24,16},{32,40},{40,32},{48,56},{56,48},{64,72... | collective-permute-start | bytes 6152 | tf_op jit(solution)/shard_map/ppermute | solution.py:59
  84.8 16.7 %collective-permute-start.10 = (f32[512]{0:T(512)S(1)}, f32[512]{0:T(512)S(1)}, u32[]{:S(2)}, u32[]{:S(2)}) collective-permute-start(f32[512]{0:T(512)S(1)} %add.194), channel_id=1, source_target_pairs={{0,64},{8,72},{16,208},{24,216},{32,224},{40,232},{48,240},{56,248... | collective-permute-start | bytes 6152 | tf_op jit(solution)/shard_map/ppermute | solution.py:59
  100.1 11.3 %copy-start.1 = (bf16[1,128,2048]{2,1,0:T(8,128)(2,1)S(1)}, bf16[1,128,2048]{2,1,0:T(8,128)(2,1)}, u32[]{:S(2)}) copy-start(bf16[1,128,2048]{2,1,0:T(8,128)(2,1)} %param.7) | copy-start | bytes 1572868
  101.5 14.0 %collective-permute-start.11 = (f32[512]{0:T(512)S(1)}, f32[512]{0:T(512)S(1)}, u32[]{:S(2)}, u32[]{:S(2)}) collective-permute-start(f32[512]{0:T(512)S(1)} %add.195), channel_id=1, source_target_pairs={{0,240},{8,248},{16,32},{24,40},{32,16},{40,24},{48,64},{56,72},{6... | collective-permute-start | bytes 6152 | tf_op jit(solution)/shard_map/ppermute | solution.py:59
  111.4 3.0 %copy-start.10 = (bf16[128,4,2,256]{0,3,2,1:T(8,128)(2,1)S(1)}, bf16[128,4,2,256]{0,3,2,1:T(8,128)(2,1)}, u32[]{:S(2)}) copy-start(bf16[128,4,2,256]{0,3,2,1:T(8,128)(2,1)} %get-tuple-element.60) | copy-start | bytes 1572868
  115.5 9.4 %collective-permute-start.12 = (f32[512]{0:T(512)S(1)}, f32[512]{0:T(512)S(1)}, u32[]{:S(2)}, u32[]{:S(2)}) collective-permute-start(f32[512]{0:T(512)S(1)} %add.200), channel_id=1, source_target_pairs={{0,192},{8,200},{16,80},{24,88},{32,96},{40,104},{48,112},{56,120}... | collective-permute-start | bytes 6152 | tf_op jit(solution)/shard_map/ppermute | solution.py:59
  124.9 7.6 %collective-permute-start.13 = (f32[512]{0:T(512)S(1)}, f32[512]{0:T(512)S(1)}, u32[]{:S(2)}, u32[]{:S(2)}) collective-permute-start(f32[512]{0:T(512)S(1)} %add.201), channel_id=1, source_target_pairs={{0,224},{8,232},{16,48},{24,56},{32,64},{40,72},{48,16},{56,24},{6... | collective-permute-start | bytes 6152 | tf_op jit(solution)/shard_map/ppermute | solution.py:59
  132.5 11.1 %copy-start.7 = (bf16[1,128,2048]{1,2,0:T(8,128)(2,1)S(1)}, bf16[1,128,2048]{1,2,0:T(8,128)(2,1)}, u32[]{:S(2)}) copy-start(bf16[1,128,2048]{1,2,0:T(8,128)(2,1)} %copy.207) | copy-start | bytes 1572868
  132.5 11.1 %copy-start.9 = (f32[4,2,128,128]{2,3,1,0:T(8,128)S(1)}, f32[4,2,128,128]{2,3,1,0:T(8,128)}, u32[]{:S(2)}) copy-start(f32[4,2,128,128]{2,3,1,0:T(8,128)} %get-tuple-element.54) | copy-start | bytes 1572868
  132.5 5.6 %collective-permute-start.14 = (f32[512]{0:T(512)S(1)}, f32[512]{0:T(512)S(1)}, u32[]{:S(2)}, u32[]{:S(2)}) collective-permute-start(f32[512]{0:T(512)S(1)} %add.202), channel_id=1, source_target_pairs={{0,256},{8,264},{16,272},{24,280},{32,288},{40,296},{48,304},{56,3... | collective-permute-start | bytes 6152 | tf_op jit(solution)/shard_map/ppermute | solution.py:59
  138.1 8.5 %collective-permute-start.15 = (f32[512]{0:T(512)S(1)}, f32[512]{0:T(512)S(1)}, u32[]{:S(2)}, u32[]{:S(2)}) collective-permute-start(f32[512]{0:T(512)S(1)} %add.203), channel_id=1, source_target_pairs={{0,768},{8,776},{16,784},{24,792},{32,800},{40,808},{48,816},{56,8... | collective-permute-start | bytes 6152 | tf_op jit(solution)/shard_map/ppermute | solution.py:59
  (8 other events, 7.0 us)

commit v3 on v2

--- a/solution.py
+++ b/solution.py
@@ -49,6 +49,19 @@
             rounds.append((axis, pairs))
             bit *= 2
     return rounds
+
+
+def tree_sum(parts):
+    while len(parts) > 1:
+        paired = [parts[i] + parts[i + 1] for i in range(0, len(parts) - 1, 2)]
+        parts = paired + parts[len(parts) - len(parts) % 2 :]
+    return parts[0]
+
+
+def group_sum(value, axis):
+    count = lax.axis_size(axis)
+    gathered = lax.all_to_all(jnp.broadcast_to(value, (count,) + value.shape), axis, 0, 0)
+    return tree_sum([gathered[i] for i in range(count)])
 
 
 def apply_rounds(value, rounds):
@@ -184,15 +197,13 @@
         jnp.sum(back_blocks[block][1].astype(jnp.float32) * key_hat_list[block], (0, 1))
         for block in range(HALO + 1)
     )
-    rounds = butterfly_rounds()
-    split = min(GAIN_ROUNDS_BEFORE_RETURN, len(rounds))
-    gain_partial = apply_rounds(jnp.concatenate([q_sum_part, k_sum_part]), rounds[:split])
+    gain_partial = group_sum(jnp.concatenate([q_sum_part, k_sum_part]), "dp")
     returned_list = [
         shifted(jnp.stack([back_blocks[HALO - offset][1], back_blocks[HALO - offset][2]]), "ctx", -offset)
         for offset in range(1, HALO + 1)
     ]
     returned_list, gain_partial = lax.optimization_barrier((returned_list, gain_partial))
-    gain_total = apply_rounds(gain_partial, rounds[split:])
+    gain_total = group_sum(gain_partial, "ctx")
     q_total, k_total = gain_total[:HEAD_SIZE], gain_total[HEAD_SIZE:]
     key_acc = back_blocks[HALO][1].astype(jnp.float32)
     value_accumulator = back_blocks[HALO][2].astype(jnp.float32)

time: 148 us -> 143 us (0.966)
  the two profiles are of different devices: /device:TPU:24 before, /device:TPU:1 now
where the time goes in v3:
time: 143 us; the launch traced here: 140 us
  starting transfers between devices  62.7 us (44%)
  waiting for transfers between devices  27.6 us (19%)
  local copies, waits for them, and re-layouts  23.7 us (17%)
  other arithmetic  14.1 us (10%)
  matrix products  10.9 us (8%)
    all_to_all x2, starting transfers between devices, group_sum(): lax.all_to_all(jnp.broadcast_to(value, (count,) + value.shape), axis, 0, 0)  42.5 us
    ppermute x6, starting transfers between devices, shifted(): return lax.ppermute(value, axis, pairs)  20.2 us
    ppermute x6, waiting for transfers between devices, shifted(): return lax.ppermute(value, axis, pairs)  16.9 us
    unnamed x44, local copies, waits for them, and re-layouts  11.9 us
    all_to_all x2, waiting for transfers between devices, group_sum(): lax.all_to_all(jnp.broadcast_to(value, (count,) + value.shape), axis, 0, 0)  10.8 us
    dot_general x3, matrix products, backward_block(): jnp.einsum('hgqk,qhgd->khd', prob_b_blocks[block], grad_out, preferred_el...  3.35 us
    convert_element_type x1, other arithmetic, body(): grad_queries = rms_norm_backward(q_grad_norm, q_normed, q_inv, q_gain).as...  3.02 us
  transfers between devices with their start and end apart: 8, of which 3 were waited for; matrix products, arithmetic and copies ran while one was open for 19% of the time, Pallas kernels for 0%

profile of v3, /device:TPU:1, one launch (start us, length us, event | category | flops | bytes accessed | tf_op | source)
XLA Modules:
  0.0 140.1 jit_solution(10677639066764600671)
XLA Ops:
  1.3 4.9 %collective-permute-start.1 = (s32[128]{0:T(128)S(1)}, s32[128]{0:T(128)S(1)}, u32[]{:S(2)}, u32[]{:S(2)}) collective-permute-start(s32[128]{0:T(128)S(1)} %bitcast.299), channel_id=1, source_target_pairs={{0,16},{8,24},{16,32},{24,40},{32,48},{40,56},{48,64},{56,72},{64,... | collective-permute-start | bytes 1544 | tf_op jit(solution)/shard_map/ppermute | solution.py:79
  6.2 3.2 %collective-permute-start.2 = (s32[128]{0:T(128)S(1)}, s32[128]{0:T(128)S(1)}, u32[]{:S(2)}, u32[]{:S(2)}) collective-permute-start(s32[128]{0:T(128)S(1)} %bitcast.300), channel_id=1, source_target_pairs={{0,8},{8,16},{16,24},{24,32},{32,40},{40,48},{48,56},{56,64},{64,7... | collective-permute-start | bytes 1544 | tf_op jit(solution)/shard_map/ppermute | solution.py:79
  9.4 1.7 %constant_dynamic-update-slice_fusion.1 = bf16[2,128,1024]{2,1,0:T(8,128)(2,1)} fusion(bf16[1,128,1024]{2,1,0:T(8,128)(2,1)} %param.8), kind=kLoop, calls=%fused_computation.109 | loop fusion | bytes 524288
  11.8 4.8 %collective-permute-start = (bf16[2,128,1024]{2,1,0:T(8,128)(2,1)}, bf16[2,128,1024]{2,1,0:T(8,128)(2,1)}, u32[]{:S(2)}, u32[]{:S(2)}) collective-permute-start(bf16[2,128,1024]{2,1,0:T(8,128)(2,1)} %constant_dynamic-update-slice_fusion), channel_id=1, source_target_pairs={{0,16},{8,24},{16,32},{24,40},{32,48},{40,56},{48,64},{56,72},{64,... | collective-permute-start | bytes 1572872 | tf_op jit(solution)/shard_map/ppermute | solution.py:79
  16.6 4.7 %collective-permute-start.3 = (bf16[2,128,1024]{2,1,0:T(8,128)(2,1)}, bf16[2,128,1024]{2,1,0:T(8,128)(2,1)}, u32[]{:S(2)}, u32[]{:S(2)}) collective-permute-start(bf16[2,128,1024]{2,1,0:T(8,128)(2,1)} %constant_dynamic-update-slice_fusion), channel_id=1, source_target_pairs={{0,8},{8,16},{16,24},{24,32},{32,40},{40,48},{48,56},{56,64},{64,7... | collective-permute-start | bytes 1572872 | tf_op jit(solution)/shard_map/ppermute | solution.py:79
  23.1 1.3 copy.289
  24.5 1.4 %reduce_sum.127 = f32[128,8]{1,0:T(8,128)S(1)} reduce(f32[128,8,256]{2,1,0:T(8,128)} %bitcast.263, f32[]{:T(128)} %constant.34.clone.1), dimensions={2}, to_apply=%region_1.0 | reduce | flops 261120 | bytes 1052676 | tf_op jit(solution)/shard_map/reduce_sum | solution.py:84
  30.5 1.2 fusion.123
  33.1 2.0 %slice_convert_fusion = (f32[1,128,1024]{2,1,0:T(8,128)}, bf16[1,128,1024]{2,1,0:T(8,128)(2,1)}) fusion(bf16[2,128,1024]{2,1,0:T(8,128)(2,1)} %collective-permute-done.3), kind=kLoop, calls=%fused_computation.85 | loop fusion | flops 131072 | bytes 1310720 | tf_op jit(solution)/shard_map/convert_element_type | solution.py:83
  35.1 1.2 copy.194
  36.4 1.8 %copy.201 = bf16[1,128,1024]{1,2,0:T(8,128)(2,1)} copy(bf16[1,128,1024]{2,1,0:T(8,128)(2,1)} %get-tuple-element.47) | data formatting | bytes 524288 | tf_op jit(solution)/shard_map/slice | solution.py:134
  50.3 8.9 %all-to-all-start = ((f32[8,1,512]{2,1,0:T(1,128)}), f32[8,1,512]{2,1,0:T(1,128)S(1)}, u32[]{:S(2)}, u32[]{:S(2)}) async-start(f32[8,1,512]{2,1,0:T(1,128)} %broadcast_in_dim.24), calls=%async_computation | async-start | bytes 32768 | tf_op jit(solution)/shard_map/all_to_all | solution.py:63
  59.2 1.8 %pad_maximum_fusion.1 = bf16[2,128,4,256]{1,3,2,0:T(8,128)(2,1)} fusion(bf16[1,128,4,256]{1,3,2,0:T(8,128)(2,1)} %fusion.35, bf16[1,128,4,256]{1,3,2,0:T(8,128)(2,1)S(1)} %bitcast.265), kind=kLoop, calls=%fused_computation.61 | loop fusion | flops 262144 | bytes 1048576 | tf_op jit(solution)/shard_map/stack | solution.py:202
  61.0 1.3 collective-permute-start.5
  63.2 1.3 collective-permute-start.4
  64.9 1.2 mul.298
  66.1 1.3 copy.217
  67.4 16.6 %collective-permute-done.5 = bf16[2,128,4,256]{1,3,2,0:T(8,128)(2,1)} collective-permute-done((bf16[2,128,4,256]{1,3,2,0:T(8,128)(2,1)}, bf16[2,128,4,256]{1,3,2,0:T(8,128)(2,1)}, u32[]{:S(2)}, u32[]{:S(2)}) %collective-permute-start.5) | collective-permute-done | bytes 524320 | tf_op jit(solution)/shard_map/ppermute | solution.py:79
  85.1 33.6 %all-to-all-start.1 = ((f32[128,1,512]{2,1,0:T(1,128)}), f32[128,1,512]{2,1,0:T(1,128)S(1)}, u32[]{:S(2)}, u32[]{:S(2)}) async-start(f32[128,1,512]{2,1,0:T(1,128)} %broadcast_in_dim.25), calls=%async_computation.1 | async-start | bytes 524288 | tf_op jit(solution)/shard_map/all_to_all | solution.py:63
  118.7 3.0 %multiply_convert_fusion = bf16[1,128,2048]{2,1,0:T(8,128)(2,1)} fusion(f32[1,128,2048]{2,1,0:T(8,128)} %mul.278, f32[1,128,2048]{2,1,0:T(8,128)} %mul.298, f32[1,128,2048]{2,1,0:T(8,128)} %copy.217, bf16[1,128,2048]{2,1,0:T(8,128)(2,1)S(1)} %copy-done.1, f32[2048]{0:T(1024)S(1)} %bitcast.284), kind=kLoop, calls=%fused_computation.57 | loop fusion | flops 1835008 | bytes 4202496 | tf_op jit(solution)/shard_map/convert_element_type | solution.py:215
  123.1 1.3 fusion.34
  125.3 1.2 multiply_reduce_fusion.1
  126.5 1.2 multiply_convert_fusion.2
  128.6 10.8 %all-to-all-done.1 = f32[128,1,512]{2,1,0:T(1,128)S(1)} async-done(((f32[128,1,512]{2,1,0:T(1,128)}), f32[128,1,512]{2,1,0:T(1,128)S(1)}, u32[]{:S(2)}, u32[]{:S(2)}) %all-to-all-start.1) | async-done | bytes 262176 | tf_op jit(solution)/shard_map/all_to_all | solution.py:63
  (104 shorter events, 27.2 us)
Async XLA Ops:
  0.6 10.5 %copy-start.3 = (bf16[1,128,1024]{2,1,0:T(8,128)(2,1)S(1)}, bf16[1,128,1024]{2,1,0:T(8,128)(2,1)}, u32[]{:S(2)}) copy-start(bf16[1,128,1024]{2,1,0:T(8,128)(2,1)} %param.9) | copy-start | bytes 786436
  1.3 20.1 %copy-start = (bf16[1,128,2048]{2,1,0:T(8,128)(2,1)S(1)}, bf16[1,128,2048]{2,1,0:T(8,128)(2,1)}, u32[]{:S(2)}) copy-start(bf16[1,128,2048]{2,1,0:T(8,128)(2,1)} %param.7) | copy-start | bytes 1572868
  1.3 28.3 %collective-permute-start.1 = (s32[128]{0:T(128)S(1)}, s32[128]{0:T(128)S(1)}, u32[]{:S(2)}, u32[]{:S(2)}) collective-permute-start(s32[128]{0:T(128)S(1)} %bitcast.299), channel_id=1, source_target_pairs={{0,16},{8,24},{16,32},{24,40},{32,48},{40,56},{48,64},{56,72},{64,... | collective-permute-start | bytes 1544 | tf_op jit(solution)/shard_map/ppermute | solution.py:79
  6.2 23.4 %collective-permute-start.2 = (s32[128]{0:T(128)S(1)}, s32[128]{0:T(128)S(1)}, u32[]{:S(2)}, u32[]{:S(2)}) collective-permute-start(s32[128]{0:T(128)S(1)} %bitcast.300), channel_id=1, source_target_pairs={{0,8},{8,16},{16,24},{24,32},{32,40},{40,48},{48,56},{56,64},{64,7... | collective-permute-start | bytes 1544 | tf_op jit(solution)/shard_map/ppermute | solution.py:79
  11.8 19.9 %collective-permute-start = (bf16[2,128,1024]{2,1,0:T(8,128)(2,1)}, bf16[2,128,1024]{2,1,0:T(8,128)(2,1)}, u32[]{:S(2)}, u32[]{:S(2)}) collective-permute-start(bf16[2,128,1024]{2,1,0:T(8,128)(2,1)} %constant_dynamic-update-slice_fusion), channel_id=1, source_target_pairs={{0,16},{8,24},{16,32},{24,40},{32,48},{40,56},{48,64},{56,72},{64,... | collective-permute-start | bytes 1572872 | tf_op jit(solution)/shard_map/ppermute | solution.py:79
  16.6 16.4 %collective-permute-start.3 = (bf16[2,128,1024]{2,1,0:T(8,128)(2,1)}, bf16[2,128,1024]{2,1,0:T(8,128)(2,1)}, u32[]{:S(2)}, u32[]{:S(2)}) collective-permute-start(bf16[2,128,1024]{2,1,0:T(8,128)(2,1)} %constant_dynamic-update-slice_fusion), channel_id=1, source_target_pairs={{0,8},{8,16},{16,24},{24,32},{32,40},{40,48},{48,56},{56,64},{64,7... | collective-permute-start | bytes 1572872 | tf_op jit(solution)/shard_map/ppermute | solution.py:79
  21.5 1.0 copy-start.2
  26.2 1.0 copy-start.6
  29.8 0.7 copy-start.15
  39.4 1.0 copy-start.13
  40.4 0.9 copy-start.5
  41.3 1.0 copy-start.7
  41.3 1.2 copy-start.9
  41.3 1.3 copy-start.12
  50.3 17.1 %all-to-all-start = ((f32[8,1,512]{2,1,0:T(1,128)}), f32[8,1,512]{2,1,0:T(1,128)S(1)}, u32[]{:S(2)}, u32[]{:S(2)}) async-start(f32[8,1,512]{2,1,0:T(1,128)} %broadcast_in_dim.24), calls=%async_computation | async-start | bytes 32768 | tf_op jit(solution)/shard_map/all_to_all | solution.py:63
  59.2 3.1 %copy-start.4 = (bf16[4,256,128]{2,1,0:T(8,128)(2,1)S(1)}, bf16[4,256,128]{2,1,0:T(8,128)(2,1)}, u32[]{:S(2)}) copy-start(bf16[4,256,128]{2,1,0:T(8,128)(2,1)} %get-tuple-element.67) | copy-start | bytes 786436
  59.2 3.2 %copy-start.14 = (bf16[1,128,4,256]{1,3,2,0:T(8,128)(2,1)S(1)}, bf16[1,128,4,256]{1,3,2,0:T(8,128)(2,1)}, u32[]{:S(2)}) copy-start(bf16[1,128,4,256]{1,3,2,0:T(8,128)(2,1)} %fusion.36) | copy-start | bytes 786436
  61.0 23.0 %collective-permute-start.5 = (bf16[2,128,4,256]{1,3,2,0:T(8,128)(2,1)}, bf16[2,128,4,256]{1,3,2,0:T(8,128)(2,1)}, u32[]{:S(2)}, u32[]{:S(2)}) collective-permute-start(bf16[2,128,4,256]{1,3,2,0:T(8,128)(2,1)} %pad_maximum_fusion.1), channel_id=1, source_target_pairs={{16,0},{24,8},{32,16},{40,24},{48,32},{56,40},{64,48},{72,56},{80,... | collective-permute-start | bytes 1572872 | tf_op jit(solution)/shard_map/ppermute | solution.py:79
  63.2 21.1 %collective-permute-start.4 = (bf16[2,128,4,256]{1,3,2,0:T(8,128)(2,1)}, bf16[2,128,4,256]{1,3,2,0:T(8,128)(2,1)}, u32[]{:S(2)}, u32[]{:S(2)}) collective-permute-start(bf16[2,128,4,256]{1,3,2,0:T(8,128)(2,1)} %pad_maximum_fusion), channel_id=1, source_target_pairs={{8,0},{16,8},{24,16},{32,24},{40,32},{48,40},{56,48},{64,56},{72,6... | collective-permute-start | bytes 1572872 | tf_op jit(solution)/shard_map/ppermute | solution.py:79
  67.4 51.3 %copy-start.1 = (bf16[1,128,2048]{2,1,0:T(8,128)(2,1)S(1)}, bf16[1,128,2048]{2,1,0:T(8,128)(2,1)}, u32[]{:S(2)}) copy-start(bf16[1,128,2048]{2,1,0:T(8,128)(2,1)} %param.7) | copy-start | bytes 1572868
  85.1 54.3 %all-to-all-start.1 = ((f32[128,1,512]{2,1,0:T(1,128)}), f32[128,1,512]{2,1,0:T(1,128)S(1)}, u32[]{:S(2)}, u32[]{:S(2)}) async-start(f32[128,1,512]{2,1,0:T(1,128)} %broadcast_in_dim.25), calls=%async_computation.1 | async-start | bytes 524288 | tf_op jit(solution)/shard_map/all_to_all | solution.py:63
  118.7 3.0 %copy-start.11 = (bf16[128,4,2,256]{0,3,2,1:T(8,128)(2,1)S(1)}, bf16[128,4,2,256]{0,3,2,1:T(8,128)(2,1)}, u32[]{:S(2)}) copy-start(bf16[128,4,2,256]{0,3,2,1:T(8,128)(2,1)} %get-tuple-element.60) | copy-start | bytes 1572868
  121.7 1.0 copy-start.8
  121.7 1.4 copy-start.10
  (2 other events, 1.3 us)

commit v4 on v3

--- a/solution.py
+++ b/solution.py
@@ -1,10 +1,8 @@
-import itertools
-import math
-
 import jax
 import jax.numpy as jnp
 from jax import lax
 from jax.sharding import PartitionSpec as P
+
 
 QUERY_HEADS = 8
 KEY_VALUE_HEADS = 4
@@ -14,41 +12,6 @@
 
 
 EPS = 1e-06
-GAIN_ROUNDS_BEFORE_RETURN = 5
-
-
-RING_ORDER = {2: (0, 1), 4: (0, 1, 3, 2), 16: (11, 7, 12, 8, 15, 3, 0, 4, 9, 5, 10, 6, 13, 1, 14, 2)}
-AXIS_PARTS = {"ctx": (4, 16, 2), "dp": (4, 2)}
-
-
-def virtual_order(axis, count):
-    parts = AXIS_PARTS.get(axis)
-    if parts is None or count != math.prod(parts) or any(p not in RING_ORDER for p in parts):
-        return list(range(count))
-    order = []
-    for digits in itertools.product(*[range(p) for p in parts]):
-        index = 0
-        for digit, size in zip(digits, parts):
-            index = index * size + RING_ORDER[size][digit]
-        order.append(index)
-    return order
-
-
-def butterfly_rounds():
-    rounds = []
-    for axis in ("dp", "ctx"):
-        count = lax.axis_size(axis)
-        if count & (count - 1):
-            rounds.append((axis, None))
-            continue
-        device_of = virtual_order(axis, count)
-        virtual_of = {device: virtual for virtual, device in enumerate(device_of)}
-        bit = 1
-        while bit < count:
-            pairs = [(device, device_of[virtual_of[device] ^ bit]) for device in range(count)]
-            rounds.append((axis, pairs))
-            bit *= 2
-    return rounds
 
 
 def tree_sum(parts):
@@ -62,15 +25,6 @@
     count = lax.axis_size(axis)
     gathered = lax.all_to_all(jnp.broadcast_to(value, (count,) + value.shape), axis, 0, 0)
     return tree_sum([gathered[i] for i in range(count)])
-
-
-def apply_rounds(value, rounds):
-    for axis, pairs in rounds:
-        if pairs is None:
-            value = lax.psum(value, axis)
-        else:
-            value = value + lax.ppermute(value, axis, pairs)
-    return value
 
 
 def shifted(value, axis, by):
@@ -168,9 +122,7 @@
     )
 
     def backward_block(block):
-        prob_grad = jnp.einsum(
-            "qhgd,khd->hgqk", grad_out, value_block_list[block], preferred_element_type=jnp.float32
-        )
+        prob_grad = jnp.einsum("qhgd,khd->hgqk", grad_out, value_block_list[block], preferred_element_type=jnp.float32)
         score_grad = (exp_blocks[block] / row_totals * (prob_grad - row_delta[..., None])).astype(
             jnp.bfloat16
         )
@@ -189,6 +141,9 @@
         return (q_part, key_term, value_term)
 
     back_blocks = [backward_block(block) for block in range(HALO + 1)]
+    value_returns = [
+        shifted(back_blocks[HALO - offset][2], "ctx", -offset) for offset in range(1, HALO + 1)
+    ]
     q_grad_norm = (sum((item[0] for item in back_blocks)) * score_scale).reshape(
         token_rows, QUERY_HEADS, HEAD_SIZE
     )
@@ -198,8 +153,12 @@
         for block in range(HALO + 1)
     )
     gain_partial = group_sum(jnp.concatenate([q_sum_part, k_sum_part]), "dp")
+    far_key_return = shifted(back_blocks[0][1], "ctx", -HALO)
     returned_list = [
-        shifted(jnp.stack([back_blocks[HALO - offset][1], back_blocks[HALO - offset][2]]), "ctx", -offset)
+        (
+            far_key_return if offset == HALO else shifted(back_blocks[HALO - offset][1], "ctx", -offset),
+            value_returns[offset - 1],
+        )
         for offset in range(1, HALO + 1)
     ]
     returned_list, gain_partial = lax.optimization_barrier((returned_list, gain_partial))

time: 143 us -> 143 us (level)
  waiting for transfers between devices: 27.6 us -> 36.4 us
  starting transfers between devices: 62.7 us -> 56.2 us
  other arithmetic: 14.1 us -> 12.4 us
    all_to_all x2, starting transfers between devices: 42.5 us -> 33.4 us  [group_sum(): lax.all_to_all(jnp.broadcast_to(value, (count,) + value.shape), axis, 0, 0)]
    ppermute x6 -> x8, waiting for transfers between devices: 16.9 us -> 23.1 us  [shifted(): return lax.ppermute(value, axis, pairs)]
    another operation x2 -> x0, other arithmetic: 2.7 us -> none  [body(): jnp.stack([back_blocks[HALO - offset][1], back_blocks[HALO - offset][2]])]
    ppermute x6 -> x8, starting transfers between devices: 20.2 us -> 22.8 us  [shifted(): return lax.ppermute(value, axis, pairs)]
    all_to_all x2, waiting for transfers between devices: 10.8 us -> 13.3 us  [group_sum(): lax.all_to_all(jnp.broadcast_to(value, (count,) + value.shape), axis, 0, 0)]
    unnamed x44 -> x42, local copies, waits for them, and re-layouts: 11.9 us -> 11.5 us
  transfers between devices with their start and end apart: 8 -> 10, of which waited for: 3 -> 4; matrix products, arithmetic and copies ran while one was open for 19% -> 18% of each run, Pallas kernels for 0% -> 0%
where the time goes in v4:
time: 143 us; the launch traced here: 141 us
  starting transfers between devices  56.2 us (39%)
  waiting for transfers between devices  36.4 us (25%)
  local copies, waits for them, and re-layouts  23.4 us (16%)
  other arithmetic  12.4 us (9%)
  matrix products  11.3 us (8%)
    all_to_all x2, starting transfers between devices, group_sum(): lax.all_to_all(jnp.broadcast_to(value, (count,) + value.shape), axis, 0, 0)  33.4 us
    ppermute x8, waiting for transfers between devices, shifted(): return lax.ppermute(value, axis, pairs)  23.1 us
    ppermute x8, starting transfers between devices, shifted(): return lax.ppermute(value, axis, pairs)  22.8 us
    all_to_all x2, waiting for transfers between devices, group_sum(): lax.all_to_all(jnp.broadcast_to(value, (count,) + value.shape), axis, 0, 0)  13.3 us
    unnamed x42, local copies, waits for them, and re-layouts  11.5 us
    dot_general x3, matrix products, backward_block(): jnp.einsum('hgqk,qhgd->khd', prob_b_blocks[block], grad_out, preferred_el...  3.12 us
    convert_element_type x1, other arithmetic, body(): grad_queries = rms_norm_backward(q_grad_norm, q_normed, q_inv, q_gain).as...  3.02 us
  transfers between devices with their start and end apart: 10, of which 4 were waited for; matrix products, arithmetic and copies ran while one was open for 18% of the time, Pallas kernels for 0%

profile of v4, /device:TPU:1, one launch (start us, length us, event | category | flops | bytes accessed | tf_op | source)
XLA Modules:
  0.0 140.8 jit_solution(3414570515893110150)
XLA Ops:
  1.3 4.9 %collective-permute-start.1 = (s32[128]{0:T(128)S(1)}, s32[128]{0:T(128)S(1)}, u32[]{:S(2)}, u32[]{:S(2)}) collective-permute-start(s32[128]{0:T(128)S(1)} %bitcast.264), channel_id=1, source_target_pairs={{0,16},{8,24},{16,32},{24,40},{32,48},{40,56},{48,64},{56,72},{64,... | collective-permute-start | bytes 1544 | tf_op jit(solution)/shard_map/ppermute | solution.py:33
  6.2 3.2 %collective-permute-start.2 = (s32[128]{0:T(128)S(1)}, s32[128]{0:T(128)S(1)}, u32[]{:S(2)}, u32[]{:S(2)}) collective-permute-start(s32[128]{0:T(128)S(1)} %bitcast.265), channel_id=1, source_target_pairs={{0,8},{8,16},{16,24},{24,32},{32,40},{40,48},{48,56},{56,64},{64,7... | collective-permute-start | bytes 1544 | tf_op jit(solution)/shard_map/ppermute | solution.py:33
  9.4 1.7 %constant_dynamic-update-slice_fusion.1 = bf16[2,128,1024]{2,1,0:T(8,128)(2,1)} fusion(bf16[1,128,1024]{2,1,0:T(8,128)(2,1)} %param.8), kind=kLoop, calls=%fused_computation.105 | loop fusion | bytes 524288
  11.8 4.8 %collective-permute-start = (bf16[2,128,1024]{2,1,0:T(8,128)(2,1)}, bf16[2,128,1024]{2,1,0:T(8,128)(2,1)}, u32[]{:S(2)}, u32[]{:S(2)}) collective-permute-start(bf16[2,128,1024]{2,1,0:T(8,128)(2,1)} %constant_dynamic-update-slice_fusion), channel_id=1, source_target_pairs={{0,16},{8,24},{16,32},{24,40},{32,48},{40,56},{48,64},{56,72},{64,... | collective-permute-start | bytes 1572872 | tf_op jit(solution)/shard_map/ppermute | solution.py:33
  16.6 4.7 %collective-permute-start.3 = (bf16[2,128,1024]{2,1,0:T(8,128)(2,1)}, bf16[2,128,1024]{2,1,0:T(8,128)(2,1)}, u32[]{:S(2)}, u32[]{:S(2)}) collective-permute-start(bf16[2,128,1024]{2,1,0:T(8,128)(2,1)} %constant_dynamic-update-slice_fusion), channel_id=1, source_target_pairs={{0,8},{8,16},{16,24},{24,32},{32,40},{40,48},{48,56},{56,64},{64,7... | collective-permute-start | bytes 1572872 | tf_op jit(solution)/shard_map/ppermute | solution.py:33
  23.1 1.3 copy.274
  24.4 1.4 %reduce_sum.127 = f32[128,8]{1,0:T(8,128)S(1)} reduce(f32[128,8,256]{2,1,0:T(8,128)} %bitcast.229, f32[]{:T(128)} %constant.34.clone.1), dimensions={2}, to_apply=%region_1.0 | reduce | flops 261120 | bytes 1052676 | tf_op jit(solution)/shard_map/reduce_sum | solution.py:38
  33.0 2.0 %slice_convert_fusion = (f32[1,128,1024]{2,1,0:T(8,128)}, bf16[1,128,1024]{2,1,0:T(8,128)(2,1)}) fusion(bf16[2,128,1024]{2,1,0:T(8,128)(2,1)} %collective-permute-done.3), kind=kLoop, calls=%fused_computation.81 | loop fusion | flops 131072 | bytes 1310720 | tf_op jit(solution)/shard_map/convert_element_type | solution.py:37
  35.0 1.2 copy.184
  36.3 1.8 %copy.191 = bf16[1,128,1024]{1,2,0:T(8,128)(2,1)} copy(bf16[1,128,1024]{2,1,0:T(8,128)(2,1)} %get-tuple-element.51) | data formatting | bytes 524288 | tf_op jit(solution)/shard_map/slice | solution.py:88
  42.5 1.2 multiply_reduce_fusion
  50.9 8.9 %all-to-all-start = ((f32[8,1,512]{2,1,0:T(1,128)}), f32[8,1,512]{2,1,0:T(1,128)S(1)}, u32[]{:S(2)}, u32[]{:S(2)}) async-start(f32[8,1,512]{2,1,0:T(1,128)} %broadcast_in_dim.24), calls=%async_computation | async-start | bytes 32768 | tf_op jit(solution)/shard_map/all_to_all | solution.py:26
  59.8 1.3 collective-permute-start.6
  61.0 1.3 collective-permute-start.4
  62.3 1.3 collective-permute-start.5
  63.6 1.3 collective-permute-start.7
  65.3 1.2 mul.298
  66.5 1.3 copy.207
  67.9 3.0 %multiply_convert_fusion = bf16[1,128,2048]{2,1,0:T(8,128)(2,1)} fusion(f32[1,128,2048]{2,1,0:T(8,128)} %mul.278, f32[1,128,2048]{2,1,0:T(8,128)} %mul.298, f32[1,128,2048]{2,1,0:T(8,128)} %copy.207, bf16[1,128,2048]{2,1,0:T(8,128)(2,1)S(1)} %copy-done.1, f32[2048]{0:T(1024)S(1)} %bitcast.249), kind=kLoop, calls=%fused_computation.56 | loop fusion | flops 1835008 | bytes 4202496 | tf_op jit(solution)/shard_map/convert_element_type | solution.py:174
  70.9 6.3 %collective-permute-done.6 = bf16[128,4,256]{0,2,1:T(8,128)(2,1)S(1)} collective-permute-done((bf16[128,4,256]{0,2,1:T(8,128)(2,1)}, bf16[128,4,256]{0,2,1:T(8,128)(2,1)S(1)}, u32[]{:S(2)}, u32[]{:S(2)}) %collective-permute-start.6) | collective-permute-done | bytes 262176 | tf_op jit(solution)/shard_map/ppermute | solution.py:33
  77.2 5.0 %collective-permute-done.5 = bf16[128,4,256]{2,0,1:T(8,128)(2,1)} collective-permute-done((bf16[128,4,256]{2,0,1:T(8,128)(2,1)}, bf16[128,4,256]{2,0,1:T(8,128)(2,1)}, u32[]{:S(2)}, u32[]{:S(2)}) %collective-permute-start.5) | collective-permute-done | bytes 262176 | tf_op jit(solution)/shard_map/ppermute | solution.py:33
  82.2 11.9 %collective-permute-done.7 = bf16[128,4,256]{2,0,1:T(8,128)(2,1)} collective-permute-done((bf16[128,4,256]{2,0,1:T(8,128)(2,1)}, bf16[128,4,256]{2,0,1:T(8,128)(2,1)}, u32[]{:S(2)}, u32[]{:S(2)}) %collective-permute-start.7) | collective-permute-done | bytes 262176 | tf_op jit(solution)/shard_map/ppermute | solution.py:33
  94.9 24.5 %all-to-all-start.1 = ((f32[128,1,512]{2,1,0:T(1,128)}), f32[128,1,512]{2,1,0:T(1,128)S(1)}, u32[]{:S(2)}, u32[]{:S(2)}) async-start(f32[128,1,512]{2,1,0:T(1,128)} %broadcast_in_dim.25), calls=%async_computation.1 | async-start | bytes 524288 | tf_op jit(solution)/shard_map/all_to_all | solution.py:26
  126.9 13.3 %all-to-all-done.1 = f32[128,1,512]{2,1,0:T(1,128)S(1)} async-done(((f32[128,1,512]{2,1,0:T(1,128)}), f32[128,1,512]{2,1,0:T(1,128)S(1)}, u32[]{:S(2)}, u32[]{:S(2)}) %all-to-all-start.1) | async-done | bytes 262176 | tf_op jit(solution)/shard_map/all_to_all | solution.py:26
  (106 shorter events, 31.0 us)
Async XLA Ops:
  0.6 10.5 %copy-start.3 = (bf16[1,128,1024]{2,1,0:T(8,128)(2,1)S(1)}, bf16[1,128,1024]{2,1,0:T(8,128)(2,1)}, u32[]{:S(2)}) copy-start(bf16[1,128,1024]{2,1,0:T(8,128)(2,1)} %param.9) | copy-start | bytes 786436
  1.3 20.0 %copy-start = (bf16[1,128,2048]{2,1,0:T(8,128)(2,1)S(1)}, bf16[1,128,2048]{2,1,0:T(8,128)(2,1)}, u32[]{:S(2)}) copy-start(bf16[1,128,2048]{2,1,0:T(8,128)(2,1)} %param.7) | copy-start | bytes 1572868
  1.3 28.3 %collective-permute-start.1 = (s32[128]{0:T(128)S(1)}, s32[128]{0:T(128)S(1)}, u32[]{:S(2)}, u32[]{:S(2)}) collective-permute-start(s32[128]{0:T(128)S(1)} %bitcast.264), channel_id=1, source_target_pairs={{0,16},{8,24},{16,32},{24,40},{32,48},{40,56},{48,64},{56,72},{64,... | collective-permute-start | bytes 1544 | tf_op jit(solution)/shard_map/ppermute | solution.py:33
  6.2 23.4 %collective-permute-start.2 = (s32[128]{0:T(128)S(1)}, s32[128]{0:T(128)S(1)}, u32[]{:S(2)}, u32[]{:S(2)}) collective-permute-start(s32[128]{0:T(128)S(1)} %bitcast.265), channel_id=1, source_target_pairs={{0,8},{8,16},{16,24},{24,32},{32,40},{40,48},{48,56},{56,64},{64,7... | collective-permute-start | bytes 1544 | tf_op jit(solution)/shard_map/ppermute | solution.py:33
  11.8 19.8 %collective-permute-start = (bf16[2,128,1024]{2,1,0:T(8,128)(2,1)}, bf16[2,128,1024]{2,1,0:T(8,128)(2,1)}, u32[]{:S(2)}, u32[]{:S(2)}) collective-permute-start(bf16[2,128,1024]{2,1,0:T(8,128)(2,1)} %constant_dynamic-update-slice_fusion), channel_id=1, source_target_pairs={{0,16},{8,24},{16,32},{24,40},{32,48},{40,56},{48,64},{56,72},{64,... | collective-permute-start | bytes 1572872 | tf_op jit(solution)/shard_map/ppermute | solution.py:33
  16.6 16.4 %collective-permute-start.3 = (bf16[2,128,1024]{2,1,0:T(8,128)(2,1)}, bf16[2,128,1024]{2,1,0:T(8,128)(2,1)}, u32[]{:S(2)}, u32[]{:S(2)}) collective-permute-start(bf16[2,128,1024]{2,1,0:T(8,128)(2,1)} %constant_dynamic-update-slice_fusion), channel_id=1, source_target_pairs={{0,8},{8,16},{16,24},{24,32},{32,40},{40,48},{48,56},{56,64},{64,7... | collective-permute-start | bytes 1572872 | tf_op jit(solution)/shard_map/ppermute | solution.py:33
  21.4 1.0 copy-start.2
  26.2 1.0 copy-start.5
  39.4 1.0 copy-start.13
  40.3 0.9 copy-start.4
  41.3 1.0 copy-start.6
  41.3 1.2 copy-start.8
  41.3 1.3 copy-start.12
  50.9 20.0 %all-to-all-start = ((f32[8,1,512]{2,1,0:T(1,128)}), f32[8,1,512]{2,1,0:T(1,128)S(1)}, u32[]{:S(2)}, u32[]{:S(2)}) async-start(f32[8,1,512]{2,1,0:T(1,128)} %broadcast_in_dim.24), calls=%async_computation | async-start | bytes 32768 | tf_op jit(solution)/shard_map/all_to_all | solution.py:26
  59.8 17.4 %collective-permute-start.6 = (bf16[128,4,256]{0,2,1:T(8,128)(2,1)}, bf16[128,4,256]{0,2,1:T(8,128)(2,1)S(1)}, u32[]{:S(2)}, u32[]{:S(2)}) collective-permute-start(bf16[128,4,256]{0,2,1:T(8,128)(2,1)} %get-tuple-element.69), channel_id=1, source_target_pairs={{16,0},{24,8},{32,16},{40,24},{48,32},{56,40},{64,48},{72,56},{80,... | collective-permute-start | bytes 786440 | tf_op jit(solution)/shard_map/ppermute | solution.py:33
  61.0 16.2 %collective-permute-start.4 = (bf16[128,4,256]{0,2,1:T(8,128)(2,1)}, bf16[128,4,256]{0,2,1:T(8,128)(2,1)}, u32[]{:S(2)}, u32[]{:S(2)}) collective-permute-start(bf16[128,4,256]{0,2,1:T(8,128)(2,1)} %get-tuple-element.71), channel_id=1, source_target_pairs={{8,0},{16,8},{24,16},{32,24},{40,32},{48,40},{56,48},{64,56},{72,6... | collective-permute-start | bytes 786440 | tf_op jit(solution)/shard_map/ppermute | solution.py:33
  62.3 19.9 %collective-permute-start.5 = (bf16[128,4,256]{2,0,1:T(8,128)(2,1)}, bf16[128,4,256]{2,0,1:T(8,128)(2,1)}, u32[]{:S(2)}, u32[]{:S(2)}) collective-permute-start(bf16[128,4,256]{2,0,1:T(8,128)(2,1)} %fusion.33), channel_id=1, source_target_pairs={{8,0},{16,8},{24,16},{32,24},{40,32},{48,40},{56,48},{64,56},{72,6... | collective-permute-start | bytes 786440 | tf_op jit(solution)/shard_map/ppermute | solution.py:33
  63.6 30.4 %collective-permute-start.7 = (bf16[128,4,256]{2,0,1:T(8,128)(2,1)}, bf16[128,4,256]{2,0,1:T(8,128)(2,1)}, u32[]{:S(2)}, u32[]{:S(2)}) collective-permute-start(bf16[128,4,256]{2,0,1:T(8,128)(2,1)} %fusion.32), channel_id=1, source_target_pairs={{16,0},{24,8},{32,16},{40,24},{48,32},{56,40},{64,48},{72,56},{80,... | collective-permute-start | bytes 786440 | tf_op jit(solution)/shard_map/ppermute | solution.py:33
  66.5 1.3 copy-start.1
  67.9 51.6 %copy-start.9 = (f32[4,2,128,128]{2,3,1,0:T(8,128)S(1)}, f32[4,2,128,128]{2,3,1,0:T(8,128)}, u32[]{:S(2)}) copy-start(f32[4,2,128,128]{2,3,1,0:T(8,128)} %get-tuple-element.58) | copy-start | bytes 1572868
  70.9 48.5 %copy-start.7 = (bf16[1,128,2048]{1,2,0:T(8,128)(2,1)S(1)}, bf16[1,128,2048]{1,2,0:T(8,128)(2,1)}, u32[]{:S(2)}) copy-start(bf16[1,128,2048]{1,2,0:T(8,128)(2,1)} %copy.197) | copy-start | bytes 1572868
  94.9 45.3 %all-to-all-start.1 = ((f32[128,1,512]{2,1,0:T(1,128)}), f32[128,1,512]{2,1,0:T(1,128)S(1)}, u32[]{:S(2)}, u32[]{:S(2)}) async-start(f32[128,1,512]{2,1,0:T(1,128)} %broadcast_in_dim.25), calls=%async_computation.1 | async-start | bytes 524288 | tf_op jit(solution)/shard_map/all_to_all | solution.py:26
  119.4 1.1 copy-start.10
  120.5 1.0 copy-start.11
  (3 other events, 2.0 us)
